TPU v7x, 256 devices: a whole 4x4x8 slice. The times are simulated.
256 devices in a mesh: ctx: 8 (over z), head: 16 (over y, x), req: 2 (over core).
Axes of the slice: x: 4, y: 4, z: 8, core: 2. Of those that a mesh axis runs over, the one named last changes fastest.
Arguments:
- x_in: bfloat16 [2, 8192, 16384], P('req', 'ctx', 'head'), may hold values from -6 to 6
- bc_in: bfloat16 [2, 8192, 4096], P('req', 'ctx'), may hold values from -0.625 to 0.625
- z_in: bfloat16 [2, 8192, 16384], P('req', 'ctx', 'head'), may hold values from -6 to 6
- dt_raw: float32 [2, 256, 8192], P('req', 'head', 'ctx'), may hold values from -6 to 6
- dt_bias: float32 [256], P('head'), may hold values from -3 to 1
- decay_rate: float32 [256], P('head'), may hold values from 1e-06 to 0.05
- skip_gain: float32 [256], P('head'), may hold values from 0.5 to 1.5
- conv_x: float32 [4, 16384], P(None, 'head'), may hold values from -3 to 3
- conv_bc: float32 [4, 4096], replicated, may hold values from -3 to 3
- ssm_pool: float32 [16, 256, 64, 256], P(('ctx', 'req'), 'head'), may hold values from -6 to 6
- conv_pool: float32 [16, 3, 16384], P(('ctx', 'req'), None, 'head'), may hold values from -6 to 6
- bc_cache: float32 [2, 3, 4096], P('req'), may hold values from -0.625 to 0.625
- owner: int32 [2, 16], P(None, 'head'), may hold values from 0 to 15, as said below
- lengths: int32 [2], replicated, may hold values from 2048 to 8192, as said below
Outputs:
- y_out: bfloat16 [2, 8192, 16384], P('req', 'ctx', 'head')
- block_states: float32 [2, 8, 256, 64, 256], P('req', 'ctx', 'head')
Inputs may be any that keep to these rules, and one draw needn't show every extreme that they name: `owner`: for every head block the requests' cached states lie in different slots. `lengths`: one request has all 8192 new tokens.
All inputs are finite; a program needn't handle non-finite values.
Results may differ from a plain program's by a relative error of at most 0.0053.
Values may be sent and summed in bfloat16 or wider, within the bound.
No kernel may reach another device: no remote copies, remote signals or barrier semaphores. Data moves between devices by JAX's collectives and lax.ppermute only.
A program may use at most 128 MiB of HBM per device.

v0:
```python
from functools import partial

import jax
import jax.numpy as jnp
from jax import lax
from jax.sharding import PartitionSpec as P

H = 256
P_SIZE = 64
N = 256
G = 8
K = 4
STRETCH = 256


HIGHEST = lax.Precision.HIGHEST


def broadcast(value, axis, root):
    mine = lax.axis_index(axis) == root
    return lax.psum(jnp.where(mine, value, jnp.zeros_like(value)), axis)


def passed_along(value, axis, steps):
    count = lax.axis_size(axis)
    initial, last = (max(0, -steps), min(count, count - steps))
    return lax.ppermute(value, axis, [(source, source + steps) for source in range(initial, last)])


def causal_conv(prev_rows, rows, taps):
    padded = jnp.concatenate([prev_rows, rows.astype(jnp.float32)], axis=0)
    count = rows.shape[0]
    total = taps[0] * padded[0:count]
    for offset in range(1, taps.shape[0]):
        total = total + taps[offset] * padded[offset : offset + count]
    return jax.nn.silu(total).astype(jnp.bfloat16)


def combine_pair(earlier, later):
    early_decay, early_state = earlier
    late_decay, late_state = later
    return (early_decay * late_decay, late_decay[:, None, None] * early_state + late_state)


def block_step(running, pieces, skip_gain):
    x_blk, b_blk, c_blk, step_blk, log_blk = pieces
    cum = jnp.cumsum(log_blk, axis=1)
    block_len = x_blk.shape[0]
    head_count = x_blk.shape[1]
    scores = jnp.einsum("qgn,sgn->gqs", c_blk, b_blk, preferred_element_type=jnp.float32)
    group_count = scores.shape[0]
    per_group = head_count // group_count
    scores_h = jnp.broadcast_to(
        scores[:, None], (group_count, per_group, block_len, block_len)
    ).reshape(head_count, block_len, block_len)
    row_ids = lax.broadcasted_iota(jnp.int32, (block_len, block_len), 0)
    col_ids = lax.broadcasted_iota(jnp.int32, (block_len, block_len), 1)
    causal = (row_ids >= col_ids)[None]
    decay_gap = jnp.where(causal, cum[:, :, None] - cum[:, None, :], 0.0)
    decay_mask = jnp.where(causal, jnp.exp(-decay_gap), 0.0)
    weights = (scores_h * decay_mask * step_blk[:, None, :]).astype(jnp.bfloat16)
    y_intra = jnp.einsum("hqs,shp->qhp", weights, x_blk, preferred_element_type=jnp.float32)
    state_view = running.reshape(group_count, per_group, running.shape[1], running.shape[2])
    y_state = jnp.einsum("qgn,gjpn->qgjp", c_blk.astype(jnp.float32), state_view, precision=HIGHEST)
    y_state = y_state.reshape(block_len, head_count, running.shape[1]) * jnp.exp(-cum).T[:, :, None]
    block_out = y_intra + y_state + skip_gain[None, :, None] * x_blk.astype(jnp.float32)
    block_end = cum[:, -1:]
    factor = step_blk * jnp.exp(-(block_end - cum))
    weighted = (x_blk.astype(jnp.float32) * factor.T[:, :, None]).astype(jnp.bfloat16)
    weighted_view = weighted.reshape(block_len, group_count, per_group, running.shape[1])
    contrib = jnp.einsum(
        "qgjp,qgn->gjpn", weighted_view, b_blk, preferred_element_type=jnp.float32
    ).reshape(running.shape)
    running = jnp.exp(-cum[:, -1])[:, None, None] * running + contrib
    return (running, block_out)


def on_device(
    x_in,
    bc_in,
    z_in,
    dt_raw,
    dt_bias,
    decay_rate,
    skip_gain,
    conv_x,
    conv_bc,
    ssm_pool,
    conv_pool,
    bc_cache,
    owner,
    lengths,
):
    ctx_pos = lax.axis_index("ctx")
    head_pos = lax.axis_index("head")
    req_pos = lax.axis_index("req")
    local_heads = dt_raw.shape[1]
    tokens = x_in.shape[1]
    at_start = ctx_pos == 0
    first_state = jnp.zeros(ssm_pool.shape[1:], jnp.float32)
    first_conv = jnp.zeros(conv_pool.shape[1:], jnp.float32)
    for request in range(lax.axis_size("req")):
        got_state, got_conv = (
            broadcast(ssm_pool, ("ctx", "req"), owner[request, 0]),
            broadcast(conv_pool, ("ctx", "req"), owner[request, 0]),
        )
        first_state = jnp.where(req_pos == request, got_state[0], first_state)
        first_conv = jnp.where(req_pos == request, got_conv[0], first_conv)
    tail_x = x_in[0, tokens - (K - 1) :, :]
    tail_bc = bc_in[0, tokens - (K - 1) :, :]
    prev_x, prev_bc = passed_along((tail_x, tail_bc), "ctx", 1)
    prev_x = jnp.where(at_start, first_conv, prev_x.astype(jnp.float32))
    prev_bc = jnp.where(at_start, bc_cache[0], prev_bc.astype(jnp.float32))
    per_group = H // G
    local_groups = max(1, local_heads // per_group)
    group_start = head_pos * local_heads // per_group
    span = local_groups * N

    def pick_groups(values):
        input_cols = lax.dynamic_slice_in_dim(values, group_start * N, span, 1)
        output_cols = lax.dynamic_slice_in_dim(values, G * N + group_start * N, span, 1)
        return jnp.concatenate([input_cols, output_cols], axis=1)

    x_conv = causal_conv(prev_x, x_in[0], conv_x)
    bc_conv = causal_conv(pick_groups(prev_bc), pick_groups(bc_in[0]), pick_groups(conv_bc))
    positions = ctx_pos * tokens + lax.iota(jnp.int32, tokens)
    live_mask = (positions < lengths[req_pos]).astype(jnp.float32)
    step_size = jax.nn.softplus(dt_raw[0] + dt_bias[:, None]) * live_mask[None, :]
    log_decay = step_size * decay_rate[:, None]
    blocks = tokens // STRETCH
    x_view = x_conv.reshape(blocks, STRETCH, local_heads, P_SIZE)
    b_view = bc_conv[:, :span].reshape(blocks, STRETCH, local_groups, N)
    c_view = bc_conv[:, span:].reshape(blocks, STRETCH, local_groups, N)
    step_view = step_size.reshape(local_heads, blocks, STRETCH).transpose(1, 0, 2)
    log_view = log_decay.reshape(local_heads, blocks, STRETCH).transpose(1, 0, 2)
    zero_state = jnp.zeros((local_heads, P_SIZE, N), jnp.float32)
    local_end, local_out = lax.scan(
        partial(block_step, skip_gain=skip_gain),
        zero_state,
        (x_view, b_view, c_view, step_view, log_view),
    )
    own_decay = jnp.exp(-jnp.sum(log_decay, axis=1))
    element_state = local_end + jnp.where(at_start, own_decay[:, None, None] * first_state, 0.0)
    prior_decay = jnp.ones_like(own_decay)
    prior_state = jnp.zeros_like(element_state)
    for hop_index in range(lax.axis_size("ctx") - 1):
        out_decay, out_state = combine_pair((prior_decay, prior_state), (own_decay, element_state))
        got_decay, got_state = passed_along((out_decay, out_state), "ctx", 1)
        prior_decay = jnp.where(at_start, 1.0, got_decay)
        prior_state = got_state
    start_state = jnp.where(at_start, first_state, prior_state)
    end_state = own_decay[:, None, None] * start_state + local_end
    cum_dev = jnp.cumsum(log_decay, axis=1)
    readout = bc_conv[:, span:].reshape(tokens, local_groups, N)
    start_view = start_state.reshape(local_groups, local_heads // local_groups, P_SIZE, N)
    carried = jnp.einsum(
        "tgn,gjpn->tgjp", readout.astype(jnp.float32), start_view, precision=HIGHEST
    )
    carried = carried.reshape(tokens, local_heads, P_SIZE) * jnp.exp(-cum_dev).T[:, :, None]
    mixed = local_out.reshape(tokens, local_heads, P_SIZE) + carried
    gate_act = jax.nn.silu(z_in[0].astype(jnp.float32)).reshape(tokens, local_heads, P_SIZE)
    gated = (
        (mixed * gate_act * live_mask[:, None, None])
        .reshape(1, tokens, local_heads * P_SIZE)
        .astype(jnp.bfloat16)
    )
    return (gated, end_state[None, None])


def solution(mesh):
    return jax.shard_map(
        on_device,
        mesh=mesh,
        in_specs=(
            P("req", "ctx", "head"),
            P("req", "ctx", None),
            P("req", "ctx", "head"),
            P("req", "head", "ctx"),
            P("head"),
            P("head"),
            P("head"),
            P(None, "head"),
            P(),
            P(("ctx", "req"), "head", None, None),
            P(("ctx", "req"), None, "head"),
            P("req", None, None),
            P(None, "head"),
            P(),
        ),
        out_specs=(P("req", "ctx", "head"), P("req", "ctx", "head", None, None)),
        check_vma=False,
    )
```

profile of v0, /device:TPU:80, one launch (start us, length us, event | category | flops | bytes accessed | tf_op | source)
XLA Modules:
  0.0 428.9 jit_solution(16780779303647972594)
XLA Ops:
  7.2 1.0 slice_bitcast_fusion
  8.2 3.8 collective-permute-start.1
  12.1 0.7 slice_bitcast_fusion.1
  12.8 5.0 %collective-permute-start = (bf16[3,1024]{1,0:T(4,128)(2,1)S(1)}, bf16[3,1024]{1,0:T(4,128)(2,1)S(1)}, u32[]{:S(2)}, u32[]{:S(2)}) collective-permute-start(bf16[3,1024]{1,0:T(4,128)(2,1)S(1)} %slice_bitcast_fusion.1), channel_id=1, source_target_pairs={{0,32},{32,64},{64,96},{96,128},{128,160},{160,192},{192,224},{1,3... | collective-permute-start | bytes 18440 | tf_op jit(solution)/shard_map/ppermute | solution.py:27
  17.8 1.3 fusion.74
  20.4 2.8 broadcast_select_fusion
  23.4 2.5 bitcast_convert_fusion
  27.8 1.3 dynamic-slice_bitcast_fusion.1
  29.1 0.8 constant_dynamic-slice_fusion.5
  30.2 1.7 maximum_convert_fusion
  31.9 41.0 %all-reduce = (f32[1,3,1024]{2,0,1:T(1,128)S(1)}, f32[1,3,1024]{2,0,1:T(1,128)S(1)}) all-reduce(f32[1,3,1024]{2,0,1:T(1,128)S(1)} %get-tuple-element.159, f32[1,3,1024]{2,0,1:T(1,128)S(1)} %get-tuple-element.158), channel_id=1, replica_groups=mesh['ctx'=8,'head'=16,'req'=2] {'ctx','req'}, use_global_device_ids=true, to_apply=%region_0.1 | all-reduce | flops 6144 | bytes 49152 | tf_op jit(solution)/shard_map/psum | solution.py:21
  73.2 7.5 %multiply_convert_fusion.5 = bf16[1024,1024]{1,0:T(8,128)(2,1)S(1)} fusion(f32[1024,1024]{1,0:T(8,128)} %bitcast_convert_fusion, f32[3,1024]{1,0:T(4,128)S(1)} %bitcast_select_fusion.3, f32[1024]{0:T(1024)S(1)} %bitcast.172, f32[1024]{0:T(1024)S(1)} %bitcast.173, f32[1024]{0:T(1024)S(1)} %bitcast.171, f32[1024]{0:T(1024)S(1)} %bitcast.170), kind=kLoop, calls=%fused_computation.69 | loop fusion | flops 15728640 | bytes 6320128 | tf_op jit(solution)/shard_map/convert_element_type | solution.py:36
  80.8 4.1 reshape.258
  84.8 6.0 %copy.45 = bf16[4,256,16,64]{1,3,2,0:T(8,128)(2,1)} copy(bf16[4,256,16,64]{3,2,1,0:T(8,128)(2,1)} %reshape.258) | data formatting | bytes 4194304
  92.0 1.2 multiply_convert_fusion.6
  93.2 1.0 fusion.72
  94.2 131.4 %while.13 = (s32[]{:T(128)}, f32[16,64,256]{2,1,0:T(8,128)S(1)}, f32[4,256,16,64]{1,0,3,2:T(4,128)}, f32[4,16,256]{2,0,1:T(4,128)S(1)}, bf16[4,256,16,64]{1,3,2,...) while((s32[]{:T(128)}, f32[16,64,256]{2,1,0:T(8,128)S(1)}, ...), condition=%wide.region_5.6_spmd.clone, body=%wide.region_2.5_spmd.clone.sunk | while | flops 1118392320 | bytes 13587600 | solution.py:137
  95.2 1.2 fusion.92
  96.4 2.6 fusion.93
  99.3 1.8 fusion.94
  101.1 1.1 copy.90
  102.2 23.5 %dynamic_update_slice.6 = f32[4,256,16,64]{1,0,3,2:T(4,128)} dynamic-update-slice(f32[4,256,16,64]{1,0,3,2:T(4,128)} %get-tuple-element.245, f32[1,256,16,64]{1,0,3,2:T(1,128)S(1)} %copy.90, s32[]{:T(128)} %get-tuple-element.243, s32[]{:T(128)} %constant.70.clone.1..sunk, s32[]{:T(128)} %constant.70.clone.1..sunk, s32[]{:T(128)} %constant.70.clone.1..sunk) | dynamic-update-slice | bytes 2097156 | tf_op jit(solution)/shard_map/while/body/jit(dynamic_update_index_in_dim)/dynamic_update_slice | solution.py:137
  125.7 1.4 convolution_add_fusion.2
  128.0 1.2 fusion.92
  129.3 2.6 fusion.93
  132.2 1.8 fusion.94
  134.0 1.1 copy.90
  135.1 23.4 %dynamic_update_slice.6 = f32[4,256,16,64]{1,0,3,2:T(4,128)} dynamic-update-slice(f32[4,256,16,64]{1,0,3,2:T(4,128)} %get-tuple-element.245, f32[1,256,16,64]{1,0,3,2:T(1,128)S(1)} %copy.90, s32[]{:T(128)} %get-tuple-element.243, s32[]{:T(128)} %constant.70.clone.1..sunk, s32[]{:T(128)} %constant.70.clone.1..sunk, s32[]{:T(128)} %constant.70.clone.1..sunk) | dynamic-update-slice | bytes 2097156 | tf_op jit(solution)/shard_map/while/body/jit(dynamic_update_index_in_dim)/dynamic_update_slice | solution.py:137
  158.5 1.4 convolution_add_fusion.2
  160.9 1.2 fusion.92
  162.1 2.6 fusion.93
  165.0 1.8 fusion.94
  166.9 1.1 copy.90
  168.0 23.4 %dynamic_update_slice.6 = f32[4,256,16,64]{1,0,3,2:T(4,128)} dynamic-update-slice(f32[4,256,16,64]{1,0,3,2:T(4,128)} %get-tuple-element.245, f32[1,256,16,64]{1,0,3,2:T(1,128)S(1)} %copy.90, s32[]{:T(128)} %get-tuple-element.243, s32[]{:T(128)} %constant.70.clone.1..sunk, s32[]{:T(128)} %constant.70.clone.1..sunk, s32[]{:T(128)} %constant.70.clone.1..sunk) | dynamic-update-slice | bytes 2097156 | tf_op jit(solution)/shard_map/while/body/jit(dynamic_update_index_in_dim)/dynamic_update_slice | solution.py:137
  191.4 1.4 convolution_add_fusion.2
  193.8 1.2 fusion.92
  195.0 2.6 fusion.93
  197.9 1.8 fusion.94
  199.7 1.1 copy.90
  200.8 23.4 %dynamic_update_slice.6 = f32[4,256,16,64]{1,0,3,2:T(4,128)} dynamic-update-slice(f32[4,256,16,64]{1,0,3,2:T(4,128)} %get-tuple-element.245, f32[1,256,16,64]{1,0,3,2:T(1,128)S(1)} %copy.90, s32[]{:T(128)} %get-tuple-element.243, s32[]{:T(128)} %constant.70.clone.1..sunk, s32[]{:T(128)} %constant.70.clone.1..sunk, s32[]{:T(128)} %constant.70.clone.1..sunk) | dynamic-update-slice | bytes 2097156 | tf_op jit(solution)/shard_map/while/body/jit(dynamic_update_index_in_dim)/dynamic_update_slice | solution.py:137
  224.3 1.4 convolution_add_fusion.2
  225.7 1.5 broadcast_add_fusion
  227.3 5.0 %collective-permute-start.2 = (f32[16,64,256]{2,1,0:T(8,128)S(1)}, f32[16,64,256]{2,1,0:T(8,128)S(1)}, u32[]{:S(2)}, u32[]{:S(2)}) collective-permute-start(f32[16,64,256]{2,1,0:T(8,128)S(1)} %get-tuple-element.135), channel_id=1, source_target_pairs={{0,32},{32,64},{64,96},{96,128},{128,160},{160,192},{192,224},{1,3... | collective-permute-start | bytes 3145736 | tf_op jit(solution)/shard_map/ppermute | solution.py:27
  232.3 23.2 %collective-permute-done.2 = f32[16,64,256]{2,1,0:T(8,128)S(1)} collective-permute-done((f32[16,64,256]{2,1,0:T(8,128)S(1)}, f32[16,64,256]{2,1,0:T(8,128)S(1)}, u32[]{:S(2)}, u32[]{:S(2)}) %collective-permute-start.2) | collective-permute-done | bytes 1048608 | tf_op jit(solution)/shard_map/ppermute | solution.py:27
  255.6 4.4 %collective-permute-start.3 = (f32[16,64,256]{2,1,0:T(8,128)S(1)}, f32[16,64,256]{2,1,0:T(8,128)S(1)}, u32[]{:S(2)}, u32[]{:S(2)}) collective-permute-start(f32[16,64,256]{2,1,0:T(8,128)S(1)} %multiply_add_fusion.5), channel_id=1, source_target_pairs={{0,32},{32,64},{64,96},{96,128},{128,160},{160,192},{192,224},{1,3... | collective-permute-start | bytes 3145736 | tf_op jit(solution)/shard_map/ppermute | solution.py:27
  260.0 23.1 %collective-permute-done.3 = f32[16,64,256]{2,1,0:T(8,128)S(1)} collective-permute-done((f32[16,64,256]{2,1,0:T(8,128)S(1)}, f32[16,64,256]{2,1,0:T(8,128)S(1)}, u32[]{:S(2)}, u32[]{:S(2)}) %collective-permute-start.3) | collective-permute-done | bytes 1048608 | tf_op jit(solution)/shard_map/ppermute | solution.py:27
  283.3 4.1 collective-permute-start.4
  287.4 22.5 %collective-permute-done.4 = f32[16,64,256]{2,1,0:T(8,128)S(1)} collective-permute-done((f32[16,64,256]{2,1,0:T(8,128)S(1)}, f32[16,64,256]{2,1,0:T(8,128)S(1)}, u32[]{:S(2)}, u32[]{:S(2)}) %collective-permute-start.4) | collective-permute-done | bytes 1048608 | tf_op jit(solution)/shard_map/ppermute | solution.py:27
  310.1 4.0 collective-permute-start.5
  314.1 21.8 %collective-permute-done.5 = f32[16,64,256]{2,1,0:T(8,128)S(1)} collective-permute-done((f32[16,64,256]{2,1,0:T(8,128)S(1)}, f32[16,64,256]{2,1,0:T(8,128)S(1)}, u32[]{:S(2)}, u32[]{:S(2)}) %collective-permute-start.5) | collective-permute-done | bytes 1048608 | tf_op jit(solution)/shard_map/ppermute | solution.py:27
  336.0 3.5 collective-permute-start.6
  339.5 21.4 %collective-permute-done.6 = f32[16,64,256]{2,1,0:T(8,128)S(1)} collective-permute-done((f32[16,64,256]{2,1,0:T(8,128)S(1)}, f32[16,64,256]{2,1,0:T(8,128)S(1)}, u32[]{:S(2)}, u32[]{:S(2)}) %collective-permute-start.6) | collective-permute-done | bytes 1048608 | tf_op jit(solution)/shard_map/ppermute | solution.py:27
  361.1 3.2 collective-permute-start.7
  364.3 20.8 %collective-permute-done.7 = f32[16,64,256]{2,1,0:T(8,128)S(1)} collective-permute-done((f32[16,64,256]{2,1,0:T(8,128)S(1)}, f32[16,64,256]{2,1,0:T(8,128)S(1)}, u32[]{:S(2)}, u32[]{:S(2)}) %collective-permute-start.7) | collective-permute-done | bytes 1048608 | tf_op jit(solution)/shard_map/ppermute | solution.py:27
  385.1 1.2 multiply_add_fusion
  386.3 2.9 collective-permute-start.8
  390.0 4.5 %reduce-window.16 = f32[16,8,128]{2,1,0:T(8,128)S(1)} reduce-window(f32[16,8,128]{2,1,0:T(8,128)S(1)} %fusion.62, f32[]{:T(128)} %constant.71.clone.1), window={size=1x1x128 pad=0_0x0_0x127_0}, to_apply=%region_9.10 | reduce-window | flops 2080768 | bytes 131076 | tf_op jit(solution)/shard_map/reduce-window.2
  395.0 3.9 copy.52
  398.9 5.8 %reshape.246 = f32[1,1024,1024]{1,2,0:T(8,128)} reshape(f32[4,256,16,64]{1,0,3,2:T(4,128)} %get-tuple-element.50) | data formatting | bytes 8388608 | tf_op jit(solution)/shard_map/reshape | solution.py:160
  404.8 5.0 %collective-permute-done.8 = f32[16,64,256]{2,1,0:T(8,128)} collective-permute-done((f32[16,64,256]{2,1,0:T(8,128)}, f32[16,64,256]{2,1,0:T(8,128)}, u32[]{:S(2)}, u32[]{:S(2)}) %collective-permute-start.8) | collective-permute-done | bytes 1048608 | tf_op jit(solution)/shard_map/ppermute | solution.py:27
  409.8 3.1 fusion.55
  412.9 2.9 fusion.49
  415.8 3.9 copy.53
  419.7 2.4 add_bitcast_fusion.1
  (117 shorter events, 10.6 us)
Async XLA Ops:
  7.2 16.2 %copy-start.7 = (bf16[1,1024,1024]{2,1,0:T(8,128)(2,1)S(1)}, bf16[1,1024,1024]{2,1,0:T(8,128)(2,1)}, u32[]{:S(2)}) copy-start(bf16[1,1024,1024]{2,1,0:T(8,128)(2,1)} %param.16) | copy-start | bytes 6291460
  7.2 218.5 %all-reduce.4.cloned.1.call-start = ((), (), s32[]{:S(2)}) async-start(), calls=%async_computation | async-start | bytes 4194304 | tf_op jit(solution)/shard_map/psum | solution.py:21
  8.2 82.6 %collective-permute-start.1 = (bf16[3,4096]{1,0:T(4,128)(2,1)S(1)}, bf16[3,4096]{1,0:T(4,128)(2,1)S(1)}, u32[]{:S(2)}, u32[]{:S(2)}) collective-permute-start(bf16[3,4096]{1,0:T(4,128)(2,1)S(1)} %slice_bitcast_fusion), channel_id=1, source_target_pairs={{0,32},{32,64},{64,96},{96,128},{128,160},{160,192},{192,224},{1,3... | collective-permute-start | bytes 73736 | tf_op jit(solution)/shard_map/ppermute | solution.py:27
  12.8 60.4 %collective-permute-start = (bf16[3,1024]{1,0:T(4,128)(2,1)S(1)}, bf16[3,1024]{1,0:T(4,128)(2,1)S(1)}, u32[]{:S(2)}, u32[]{:S(2)}) collective-permute-start(bf16[3,1024]{1,0:T(4,128)(2,1)S(1)} %slice_bitcast_fusion.1), channel_id=1, source_target_pairs={{0,32},{32,64},{64,96},{96,128},{128,160},{160,192},{192,224},{1,3... | collective-permute-start | bytes 18440 | tf_op jit(solution)/shard_map/ppermute | solution.py:27
  23.3 2.6 copy-start.15
  23.3 6.5 %copy-start.12 = (f32[1,3,1024]{2,0,1:T(1,128)S(1)}, f32[1,3,1024]{2,0,1:T(1,128)}, u32[]{:S(2)}) copy-start(f32[1,3,1024]{2,0,1:T(1,128)} %param.26) | copy-start | bytes 36868
  23.3 6.6 %copy-start.10 = (f32[4,1024]{1,0:T(4,128)S(1)}, f32[4,1024]{1,0:T(4,128)}, u32[]{:S(2)}) copy-start(f32[4,1024]{1,0:T(4,128)} %param.23) | copy-start | bytes 49156
  23.4 6.6 %copy-start.8 = (f32[1,16,1024]{2,1,0:T(8,128)S(1)}, f32[1,16,1024]{2,1,0:T(8,128)}, u32[]{:S(2)}) copy-start(f32[1,16,1024]{2,1,0:T(8,128)} %param.19) | copy-start | bytes 196612
  23.4 6.6 %copy-start.13 = (f32[16]{0:T(128)S(1)}, f32[16]{0:T(128)}, u32[]{:S(2)}) copy-start(f32[16]{0:T(128)} %param.20) | copy-start | bytes 196
  23.4 6.6 %copy-start.14 = (f32[16]{0:T(128)S(1)}, f32[16]{0:T(128)}, u32[]{:S(2)}) copy-start(f32[16]{0:T(128)} %param.21) | copy-start | bytes 196
  29.1 44.1 %copy-start.3 = (bf16[1024,256]{1,0:T(8,128)(2,1)}, bf16[1024,256]{1,0:T(8,128)(2,1)S(1)}, u32[]{:S(2)}) copy-start(bf16[1024,256]{1,0:T(8,128)(2,1)S(1)} %get-tuple-element.142) | copy-start | bytes 1572868
  29.1 44.1 %copy-start.5 = (bf16[1024,256]{1,0:T(8,128)(2,1)}, bf16[1024,256]{1,0:T(8,128)(2,1)S(1)}, u32[]{:S(2)}) copy-start(bf16[1024,256]{1,0:T(8,128)(2,1)S(1)} %get-tuple-element.143) | copy-start | bytes 1572868
  84.8 6.0 %copy-start.9 = (f32[1,3,4096]{2,0,1:T(1,128)S(1)}, f32[1,3,4096]{2,0,1:T(1,128)}, u32[]{:S(2)}) copy-start(f32[1,3,4096]{2,0,1:T(1,128)} %param.27) | copy-start | bytes 147460
  84.8 6.1 %copy-start.1 = (f32[1024,512]{1,0:T(8,128)S(1)}, f32[1024,512]{1,0:T(8,128)}, u32[]{:S(2)}) copy-start(f32[1024,512]{1,0:T(8,128)} %maximum_convert_fusion) | copy-start | bytes 6291460
  90.8 1.0 copy-start.4
  90.8 1.2 copy-start.6
  92.0 2.2 copy-start.11
  227.3 28.2 %collective-permute-start.2 = (f32[16,64,256]{2,1,0:T(8,128)S(1)}, f32[16,64,256]{2,1,0:T(8,128)S(1)}, u32[]{:S(2)}, u32[]{:S(2)}) collective-permute-start(f32[16,64,256]{2,1,0:T(8,128)S(1)} %get-tuple-element.135), channel_id=1, source_target_pairs={{0,32},{32,64},{64,96},{96,128},{128,160},{160,192},{192,224},{1,3... | collective-permute-start | bytes 3145736 | tf_op jit(solution)/shard_map/ppermute | solution.py:27
  255.6 27.5 %collective-permute-start.3 = (f32[16,64,256]{2,1,0:T(8,128)S(1)}, f32[16,64,256]{2,1,0:T(8,128)S(1)}, u32[]{:S(2)}, u32[]{:S(2)}) collective-permute-start(f32[16,64,256]{2,1,0:T(8,128)S(1)} %multiply_add_fusion.5), channel_id=1, source_target_pairs={{0,32},{32,64},{64,96},{96,128},{128,160},{160,192},{192,224},{1,3... | collective-permute-start | bytes 3145736 | tf_op jit(solution)/shard_map/ppermute | solution.py:27
  283.3 26.6 %collective-permute-start.4 = (f32[16,64,256]{2,1,0:T(8,128)S(1)}, f32[16,64,256]{2,1,0:T(8,128)S(1)}, u32[]{:S(2)}, u32[]{:S(2)}) collective-permute-start(f32[16,64,256]{2,1,0:T(8,128)S(1)} %multiply_add_fusion.4), channel_id=1, source_target_pairs={{0,32},{32,64},{64,96},{96,128},{128,160},{160,192},{192,224},{1,3... | collective-permute-start | bytes 3145736 | tf_op jit(solution)/shard_map/ppermute | solution.py:27
  310.1 25.7 %collective-permute-start.5 = (f32[16,64,256]{2,1,0:T(8,128)S(1)}, f32[16,64,256]{2,1,0:T(8,128)S(1)}, u32[]{:S(2)}, u32[]{:S(2)}) collective-permute-start(f32[16,64,256]{2,1,0:T(8,128)S(1)} %multiply_add_fusion.3), channel_id=1, source_target_pairs={{0,32},{32,64},{64,96},{96,128},{128,160},{160,192},{192,224},{1,3... | collective-permute-start | bytes 3145736 | tf_op jit(solution)/shard_map/ppermute | solution.py:27
  336.0 24.9 %collective-permute-start.6 = (f32[16,64,256]{2,1,0:T(8,128)S(1)}, f32[16,64,256]{2,1,0:T(8,128)S(1)}, u32[]{:S(2)}, u32[]{:S(2)}) collective-permute-start(f32[16,64,256]{2,1,0:T(8,128)S(1)} %multiply_add_fusion.2), channel_id=1, source_target_pairs={{0,32},{32,64},{64,96},{96,128},{128,160},{160,192},{192,224},{1,3... | collective-permute-start | bytes 3145736 | tf_op jit(solution)/shard_map/ppermute | solution.py:27
  361.1 24.0 %collective-permute-start.7 = (f32[16,64,256]{2,1,0:T(8,128)S(1)}, f32[16,64,256]{2,1,0:T(8,128)S(1)}, u32[]{:S(2)}, u32[]{:S(2)}) collective-permute-start(f32[16,64,256]{2,1,0:T(8,128)S(1)} %multiply_add_fusion.1), channel_id=1, source_target_pairs={{0,32},{32,64},{64,96},{96,128},{128,160},{160,192},{192,224},{1,3... | collective-permute-start | bytes 3145736 | tf_op jit(solution)/shard_map/ppermute | solution.py:27
  386.3 23.5 %collective-permute-start.8 = (f32[16,64,256]{2,1,0:T(8,128)}, f32[16,64,256]{2,1,0:T(8,128)}, u32[]{:S(2)}, u32[]{:S(2)}) collective-permute-start(f32[16,64,256]{2,1,0:T(8,128)} %multiply_add_fusion), channel_id=1, source_target_pairs={{0,32},{32,64},{64,96},{96,128},{128,160},{160,192},{192,224},{1,3... | collective-permute-start | bytes 3145736 | tf_op jit(solution)/shard_map/ppermute | solution.py:27
  404.7 8.1 %copy-start = (f32[1,1024,1024]{1,2,0:T(8,128)S(1)}, f32[1,1024,1024]{1,2,0:T(8,128)}, u32[]{:S(2)}) copy-start(f32[1,1024,1024]{1,2,0:T(8,128)} %reshape.246) | copy-start | bytes 12582916
  404.7 8.1 %copy-start.2 = (bf16[1,1024,1024]{1,2,0:T(8,128)(2,1)S(1)}, bf16[1,1024,1024]{1,2,0:T(8,128)(2,1)}, u32[]{:S(2)}) copy-start(bf16[1,1024,1024]{1,2,0:T(8,128)(2,1)} %copy.52) | copy-start | bytes 6291460
Sparse Core Ops, SparseCore 0:
  23.4 112.7 all-reduce.3
where the time goes:
time: 432 us; the launch traced here: 429 us
  waiting for transfers between devices  138 us (32%)
  local copies, waits for them, and re-layouts  131 us (30%)
  blocking collectives  41 us (9%)
  starting transfers between devices  36 us (8%)
  other arithmetic  35.3 us (8%)
  matrix products  31.2 us (7%)
  between operations  15.9 us (4%)
    ppermute x9, waiting for transfers between devices, passed_along(): lax.ppermute(value, axis, [(source, source + steps) for source in range(i...  138 us
    dynamic_update_slice x8, local copies, waits for them, and re-layouts, on_device(): lax.scan(partial(block_step, skip_gain=skip_gain), zero_state, (x_view, b...  98.1 us
    psum x1, blocking collectives, broadcast(): return lax.psum(jnp.where(mine, value, jnp.zeros_like(value)), axis)  41 us
    ppermute x9, starting transfers between devices, passed_along(): lax.ppermute(value, axis, [(source, source + steps) for source in range(i...  35.9 us
    unnamed x37, local copies, waits for them, and re-layouts  14.8 us
    dot_general x4, matrix products, block_step(): jnp.einsum('hqs,shp->qhp', weights, x_blk, preferred_element_type=jnp.flo...  10.4 us
    convert_element_type x2, other arithmetic, causal_conv(): return jax.nn.silu(total).astype(jnp.bfloat16)  8.75 us
  transfers between devices with their start and end apart: 10, of which 7 were waited for; matrix products, arithmetic and copies ran while one was open for 42% of the time, Pallas kernels for 0%

commit v1 on v0

--- a/solution.py
+++ b/solution.py
@@ -11,14 +11,10 @@
 G = 8
 K = 4
 STRETCH = 256
+CHUNKS = 4
 
 
 HIGHEST = lax.Precision.HIGHEST
-
-
-def broadcast(value, axis, root):
-    mine = lax.axis_index(axis) == root
-    return lax.psum(jnp.where(mine, value, jnp.zeros_like(value)), axis)
 
 
 def passed_along(value, axis, steps):
@@ -36,15 +32,21 @@
     return jax.nn.silu(total).astype(jnp.bfloat16)
 
 
-def combine_pair(earlier, later):
-    early_decay, early_state = earlier
-    late_decay, late_state = later
-    return (early_decay * late_decay, late_decay[:, None, None] * early_state + late_state)
-
-
-def block_step(running, pieces, skip_gain):
-    x_blk, b_blk, c_blk, step_blk, log_blk = pieces
-    cum = jnp.cumsum(log_blk, axis=1)
+def block_state(running, x_blk, b_blk, step_blk, cum):
+    block_len, head_count = x_blk.shape[0], x_blk.shape[1]
+    group_count = b_blk.shape[1]
+    per_group = head_count // group_count
+    block_end = cum[:, -1:]
+    factor = step_blk * jnp.exp(-(block_end - cum))
+    weighted = (x_blk.astype(jnp.float32) * factor.T[:, :, None]).astype(jnp.bfloat16)
+    weighted_view = weighted.reshape(block_len, group_count, per_group, running.shape[1])
+    contrib = jnp.einsum(
+        "qgjp,qgn->gjpn", weighted_view, b_blk, preferred_element_type=jnp.float32
+    ).reshape(running.shape)
+    return jnp.exp(-cum[:, -1])[:, None, None] * running + contrib
+
+
+def block_output(running, x_blk, b_blk, c_blk, step_blk, cum, skip_gain):
     block_len = x_blk.shape[0]
     head_count = x_blk.shape[1]
     scores = jnp.einsum("qgn,sgn->gqs", c_blk, b_blk, preferred_element_type=jnp.float32)
@@ -63,16 +65,7 @@
     state_view = running.reshape(group_count, per_group, running.shape[1], running.shape[2])
     y_state = jnp.einsum("qgn,gjpn->qgjp", c_blk.astype(jnp.float32), state_view, precision=HIGHEST)
     y_state = y_state.reshape(block_len, head_count, running.shape[1]) * jnp.exp(-cum).T[:, :, None]
-    block_out = y_intra + y_state + skip_gain[None, :, None] * x_blk.astype(jnp.float32)
-    block_end = cum[:, -1:]
-    factor = step_blk * jnp.exp(-(block_end - cum))
-    weighted = (x_blk.astype(jnp.float32) * factor.T[:, :, None]).astype(jnp.bfloat16)
-    weighted_view = weighted.reshape(block_len, group_count, per_group, running.shape[1])
-    contrib = jnp.einsum(
-        "qgjp,qgn->gjpn", weighted_view, b_blk, preferred_element_type=jnp.float32
-    ).reshape(running.shape)
-    running = jnp.exp(-cum[:, -1])[:, None, None] * running + contrib
-    return (running, block_out)
+    return y_intra + y_state + skip_gain[None, :, None] * x_blk.astype(jnp.float32)
 
 
 def on_device(
@@ -91,21 +84,28 @@
     owner,
     lengths,
 ):
+    n_ctx = lax.axis_size("ctx")
+    n_req = lax.axis_size("req")
     ctx_pos = lax.axis_index("ctx")
     head_pos = lax.axis_index("head")
     req_pos = lax.axis_index("req")
     local_heads = dt_raw.shape[1]
     tokens = x_in.shape[1]
     at_start = ctx_pos == 0
-    first_state = jnp.zeros(ssm_pool.shape[1:], jnp.float32)
-    first_conv = jnp.zeros(conv_pool.shape[1:], jnp.float32)
-    for request in range(lax.axis_size("req")):
-        got_state, got_conv = (
-            broadcast(ssm_pool, ("ctx", "req"), owner[request, 0]),
-            broadcast(conv_pool, ("ctx", "req"), owner[request, 0]),
-        )
-        first_state = jnp.where(req_pos == request, got_state[0], first_state)
-        first_conv = jnp.where(req_pos == request, got_conv[0], first_conv)
+
+    want = owner[req_pos, 0]
+    on_chip = (want // n_req) == ctx_pos
+    pick = want % n_req
+    swap = [(src, n_req - 1 - src) for src in range(n_req)]
+    other_pool, other_conv = lax.ppermute((ssm_pool[0], conv_pool[0]), "req", swap)
+    mine = pick == req_pos
+    first_conv = lax.psum(
+        jnp.where(on_chip, jnp.where(mine, conv_pool[0], other_conv), 0.0), "ctx"
+    )
+    first_state = lax.psum(
+        jnp.where(on_chip, jnp.where(mine, ssm_pool[0], other_pool), 0.0), "ctx"
+    )
+
     tail_x = x_in[0, tokens - (K - 1) :, :]
     tail_bc = bc_in[0, tokens - (K - 1) :, :]
     prev_x, prev_bc = passed_along((tail_x, tail_bc), "ctx", 1)
@@ -133,23 +133,53 @@
     c_view = bc_conv[:, span:].reshape(blocks, STRETCH, local_groups, N)
     step_view = step_size.reshape(local_heads, blocks, STRETCH).transpose(1, 0, 2)
     log_view = log_decay.reshape(local_heads, blocks, STRETCH).transpose(1, 0, 2)
-    zero_state = jnp.zeros((local_heads, P_SIZE, N), jnp.float32)
-    local_end, local_out = lax.scan(
-        partial(block_step, skip_gain=skip_gain),
-        zero_state,
-        (x_view, b_view, c_view, step_view, log_view),
-    )
+    cum_view = jnp.cumsum(log_view, axis=2)
+
+    running = jnp.zeros((local_heads, P_SIZE, N), jnp.float32)
+    starts = []
+    for blk in range(blocks):
+        starts.append(running)
+        running = block_state(running, x_view[blk], b_view[blk], step_view[blk], cum_view[blk])
+    local_end = running
     own_decay = jnp.exp(-jnp.sum(log_decay, axis=1))
-    element_state = local_end + jnp.where(at_start, own_decay[:, None, None] * first_state, 0.0)
-    prior_decay = jnp.ones_like(own_decay)
-    prior_state = jnp.zeros_like(element_state)
-    for hop_index in range(lax.axis_size("ctx") - 1):
-        out_decay, out_state = combine_pair((prior_decay, prior_state), (own_decay, element_state))
-        got_decay, got_state = passed_along((out_decay, out_state), "ctx", 1)
-        prior_decay = jnp.where(at_start, 1.0, got_decay)
-        prior_state = got_state
-    start_state = jnp.where(at_start, first_state, prior_state)
+
+    chunk = local_heads // CHUNKS
+    end_chunks = local_end.reshape(CHUNKS, chunk, P_SIZE, N)
+    decay_chunks = own_decay.reshape(CHUNKS, chunk)
+    got = jnp.zeros((chunk, P_SIZE, N), jnp.float32)
+    received = []
+    for step in range(n_ctx + CHUNKS - 2):
+        index = jnp.clip(step - ctx_pos, 0, CHUNKS - 1)
+        sent = (
+            lax.dynamic_index_in_dim(decay_chunks, index, keepdims=False)[:, None, None] * got
+            + lax.dynamic_index_in_dim(end_chunks, index, keepdims=False)
+        )
+        pairs = [
+            (src, src + 1)
+            for src in range(max(0, step - CHUNKS + 1), min(step, n_ctx - 2) + 1)
+        ]
+        got = lax.ppermute(sent, "ctx", pairs)
+        received.append(got)
+    received = jnp.stack(received)
+    prefix = lax.dynamic_slice_in_dim(received, jnp.maximum(ctx_pos - 1, 0), CHUNKS, 0)
+    prefix = jnp.where(at_start, 0.0, prefix.reshape(local_heads, P_SIZE, N))
+
+    all_decay = lax.all_gather(own_decay, "ctx")
+    earlier = (lax.iota(jnp.int32, n_ctx) < ctx_pos)[:, None]
+    decay_before = jnp.prod(jnp.where(earlier, all_decay, 1.0), axis=0)
+    start_state = prefix + decay_before[:, None, None] * first_state
     end_state = own_decay[:, None, None] * start_state + local_end
+
+    outs = []
+    for blk in range(blocks):
+        outs.append(
+            block_output(
+                starts[blk], x_view[blk], b_view[blk], c_view[blk], step_view[blk],
+                cum_view[blk], skip_gain,
+            )
+        )
+    local_out = jnp.concatenate(outs, axis=0)
+
     cum_dev = jnp.cumsum(log_decay, axis=1)
     readout = bc_conv[:, span:].reshape(tokens, local_groups, N)
     start_view = start_state.reshape(local_groups, local_heads // local_groups, P_SIZE, N)
@@ -157,7 +187,7 @@
         "tgn,gjpn->tgjp", readout.astype(jnp.float32), start_view, precision=HIGHEST
     )
     carried = carried.reshape(tokens, local_heads, P_SIZE) * jnp.exp(-cum_dev).T[:, :, None]
-    mixed = local_out.reshape(tokens, local_heads, P_SIZE) + carried
+    mixed = local_out + carried
     gate_act = jax.nn.silu(z_in[0].astype(jnp.float32)).reshape(tokens, local_heads, P_SIZE)
     gated = (
         (mixed * gate_act * live_mask[:, None, None])

time: 432 us -> 271 us (0.63)
  the two profiles are of different devices: /device:TPU:80 before, /device:TPU:246 now
where the time goes in v1:
time: 271 us; the launch traced here: 266 us
  waiting for transfers between devices  101 us (37%)
  other arithmetic  47 us (17%)
  blocking collectives  36.4 us (13%)
  local copies, waits for them, and re-layouts  33.5 us (12%)
  between operations  18.6 us (7%)
  matrix products  16.5 us (6%)
  starting transfers between devices  12.8 us (5%)
    ppermute x10, waiting for transfers between devices, on_device(): got = lax.ppermute(sent, 'ctx', pairs)  59.9 us
    psum x1, waiting for transfers between devices, on_device(): lax.psum(jnp.where(on_chip, jnp.where(mine, ssm_pool[0], other_pool), 0.0...  41.1 us
    psum x1, blocking collectives, on_device(): lax.psum(jnp.where(on_chip, jnp.where(mine, conv_pool[0], other_conv), 0....  36.4 us
    unnamed x151, local copies, waits for them, and re-layouts  23.4 us
    convert_element_type x2, other arithmetic, causal_conv(): return jax.nn.silu(total).astype(jnp.bfloat16)  11.9 us
    ppermute x10, starting transfers between devices, on_device(): got = lax.ppermute(sent, 'ctx', pairs)  9.57 us
    dot_general x4, matrix products, block_output(): jnp.einsum('hqs,shp->qhp', weights, x_blk, preferred_element_type=jnp.flo...  7.89 us
    another operation x5, other arithmetic  6.93 us
  transfers between devices with their start and end apart: 15, of which 5 were waited for; matrix products, arithmetic and copies ran while one was open for 31% of the time, Pallas kernels for 0%

profile of v1, /device:TPU:246, one launch (start us, length us, event | category | flops | bytes accessed | tf_op | source)
XLA Modules:
  0.0 265.8 jit_solution(10339681194358563904)
XLA Ops:
  7.2 1.5 slice_bitcast_fusion.3
  8.7 1.3 collective-permute-start.2
  10.0 1.7 copy.66
  11.7 2.9 %copy.67 = bf16[1,1024,1024]{1,2,0:T(8,128)(2,1)S(1)} copy(bf16[1,1024,1024]{2,1,0:T(8,128)(2,1)} %param.14) | data formatting | bytes 4194304 | tf_op args[0]
  14.6 0.9 slice_bitcast_fusion.2
  15.5 1.3 collective-permute-start.1
  17.4 2.4 bitcast_convert_fusion
  22.8 2.3 reduce-window.14
  30.4 1.3 dynamic-slice_bitcast_fusion.1
  31.7 0.7 constant_dynamic-slice_fusion.13
  34.8 4.5 %reduce-window.16 = f32[16,8,128]{2,1,0:T(8,128)S(1)} reduce-window(f32[16,8,128]{2,1,0:T(8,128)S(1)} %fusion.106, f32[]{:T(128)} %constant.140.clone.1), window={size=1x1x128 pad=0_0x0_0x127_0}, to_apply=%region_6.7 | reduce-window | flops 2080768 | bytes 131076 | tf_op jit(solution)/shard_map/reduce-window.2
  39.7 1.6 maximum_convert_fusion
  45.4 0.7 exp.163
  46.1 0.7 mul.623
  46.8 2.6 copy.78
  49.4 1.1 select_select_fusion.1
  50.5 36.4 %all-reduce.1 = (f32[3,1024]{0,1:T(8,128)S(1)}, f32[128]{0:T(128)S(1)}) all-reduce(f32[3,1024]{0,1:T(8,128)S(1)} %select_select_fusion.1, f32[128]{0:T(128)S(1)} %copy-done.61), channel_id=1, replica_groups=mesh['ctx'=8,'head'=16,'req'=2] {'ctx'}, use_global_device_ids=true, to_apply=%region_0.1 | all-reduce | flops 3200 | bytes 25600 | tf_op jit(solution)/shard_map/psum | solution.py:102
  86.9 1.0 convert_select_fusion
  87.9 10.7 %multiply_convert_fusion.4 = bf16[1024,1024]{0,1:T(8,128)(2,1)S(1)} fusion(f32[1024,1024]{0,1:T(8,128)} %bitcast_convert_fusion, f32[3,1024]{0,1:T(8,128)S(1)} %convert_select_fusion, f32[1024]{0:T(1024)S(1)} %bitcast.369, f32[1024]{0:T(1024)S(1)} %bitcast.370, f32[1024]{0:T(1024)S(1)} %bitcast.368, f32[1024]{0:T(1024)S(1)} %bitcast.367), kind=kLoop, calls=%fused_computation.26 | loop fusion | flops 15728640 | bytes 6320128 | tf_op jit(solution)/shard_map/convert_element_type | solution.py:32
  98.6 1.5 fusion.133
  101.3 0.8 bitcast_select_fusion
  102.4 1.2 multiply_convert_fusion.9
  106.0 0.7 collective-permute-start.3
  106.7 1.4 fusion.47
  108.2 2.5 fusion.46
  111.1 0.7 collective-permute-start.4
  111.8 2.6 fusion.45
  114.7 0.7 collective-permute-start.5
  115.5 1.4 fusion.48
  117.0 0.7 collective-permute-start.6
  117.7 1.7 fusion.58
  119.5 0.9 collective-permute-start.7
  120.5 1.6 fusion.57
  122.1 0.7 bitcast_dynamic-update-slice_fusion.9
  122.9 0.7 collective-permute-start.8
  123.6 0.7 bitcast_dynamic-update-slice_fusion.8
  124.3 0.7 bitcast_dynamic-update-slice_fusion.7
  125.1 0.7 copy-done.19
  125.8 0.8 bitcast_add_fusion.4
  126.6 1.3 collective-permute-start.9
  127.9 2.4 select_select_fusion
  130.3 39.5 %collective-permute-done.9 = f32[4,64,256]{2,1,0:T(8,128)} collective-permute-done((f32[4,64,256]{2,1,0:T(8,128)}, f32[4,64,256]{2,1,0:T(8,128)}, u32[]{:S(2)}, u32[]{:S(2)}) %collective-permute-start.9) | collective-permute-done | bytes 262176 | tf_op jit(solution)/shard_map/ppermute | solution.py:161
  169.9 1.1 bitcast_add_fusion.3
  170.9 1.3 collective-permute-start.10
  172.2 0.7 bitcast_dynamic-update-slice_fusion.6
  172.9 1.7 bitcast_dynamic-update-slice_fusion.5
  174.6 5.4 %collective-permute-done.10 = f32[4,64,256]{2,1,0:T(8,128)S(1)} collective-permute-done((f32[4,64,256]{2,1,0:T(8,128)S(1)}, f32[4,64,256]{2,1,0:T(8,128)S(1)}, u32[]{:S(2)}, u32[]{:S(2)}) %collective-permute-start.10) | collective-permute-done | bytes 262176 | tf_op jit(solution)/shard_map/ppermute | solution.py:161
  180.1 1.3 collective-permute-start.11
  181.4 1.7 bitcast_dynamic-update-slice_fusion.4
  183.0 1.7 bitcast_dynamic-update-slice_fusion.3
  184.7 6.2 %collective-permute-done.11 = f32[4,64,256]{2,1,0:T(8,128)S(1)} collective-permute-done((f32[4,64,256]{2,1,0:T(8,128)S(1)}, f32[4,64,256]{2,1,0:T(8,128)S(1)}, u32[]{:S(2)}, u32[]{:S(2)}) %collective-permute-start.11) | collective-permute-done | bytes 262176 | tf_op jit(solution)/shard_map/ppermute | solution.py:161
  191.0 1.4 collective-permute-start.12
  192.4 0.7 bitcast_dynamic-update-slice_fusion.2
  193.2 0.7 bitcast_dynamic-update-slice_fusion.1
  193.9 8.8 %collective-permute-done.12 = f32[4,64,256]{2,1,0:T(8,128)S(1)} collective-permute-done((f32[4,64,256]{2,1,0:T(8,128)S(1)}, f32[4,64,256]{2,1,0:T(8,128)S(1)}, u32[]{:S(2)}, u32[]{:S(2)}) %collective-permute-start.12) | collective-permute-done | bytes 262176 | tf_op jit(solution)/shard_map/ppermute | solution.py:161
  202.7 0.7 bitcast_dynamic-update-slice_fusion
  203.4 2.4 dynamic-slice_select_fusion
  205.8 41.1 %all-reduce.4.cloned.1.call-done = f32[16,64,256]{2,1,0:T(8,128)} async-done(((f32[16,64,256]{2,1,0:T(8,128)}), f32[16,64,256]{2,1,0:T(8,128)}) %all-reduce.4.cloned.1.call-update) | async-done | bytes 1048592 | tf_op jit(solution)/shard_map/psum | solution.py:105
  246.9 3.5 %add_bitcast_fusion = (f32[1,1,16,64,256]{4,3,2,1,0:T(8,128)}, f32[16,64,256]{2,1,0:T(8,128)S(1)}, f32[16,64,256]{2,1,0:T(8,128)S(1)}) fusion(f32[16,64,256]{2,1,0:T(8,128)} %copy-done.6, f32[16]{0:T(128)S(1)} %copy-done.56, f32[16]{0:T(128)S(1)} %copy-done.44, f32[16,64,256]{2,1,0:T(8,128)S(1)} %fusion.72, f32[16]{0:T(128)S(1)} %copy-done.59, ...), kind=kLoop, calls=%fused_computation.95 | loop fusion | flops 2883584 | bytes 9437568 | tf_op jit(solution)/shard_map/broadcast_in_dim | solution.py:197
  250.5 1.8 fusion.66
  252.4 0.7 fusion.59
  253.1 0.8 fusion.60
  254.5 1.9 fusion.13
  256.4 2.6 copy.79
  (220 shorter events, 17.8 us)
Async XLA Ops:
  7.2 34.9 %copy-start = (s32[2,1]{0,1:T(1,128)S(1)}, s32[2,1]{0,1:T(1,128)}, u32[]{:S(2)}) copy-start(s32[2,1]{0,1:T(1,128)} %param.26) | copy-start | bytes 28
  7.2 239.7 %all-reduce.4.cloned.1.call-start = ((), (), s32[]{:S(2)}) async-start(), calls=%async_computation | async-start | bytes 2097152 | tf_op jit(solution)/shard_map/psum | solution.py:105
  8.7 92.6 %collective-permute-start.2 = (bf16[3,4096]{1,0:T(4,128)(2,1)}, bf16[3,4096]{1,0:T(4,128)(2,1)}, u32[]{:S(2)}, u32[]{:S(2)}) collective-permute-start(bf16[3,4096]{1,0:T(4,128)(2,1)} %slice_bitcast_fusion.3), channel_id=1, source_target_pairs={{0,32},{32,64},{64,96},{96,128},{128,160},{160,192},{192,224},{1,3... | collective-permute-start | bytes 73736 | tf_op jit(solution)/shard_map/ppermute | solution.py:23
  11.7 37.6 %collective-permute-start = (f32[3,1024]{0,1:T(8,128)}, f32[3,1024]{0,1:T(8,128)}, u32[]{:S(2)}, u32[]{:S(2)}) collective-permute-start(f32[3,1024]{0,1:T(8,128)} %bitcast.2), channel_id=1, source_target_pairs={{0,1},{1,0},{2,3},{3,2},{4,5},{5,4},{6,7},{7,6},{8,9},{9,8},{10,11... | collective-permute-start | bytes 36872 | tf_op jit(solution)/shard_map/ppermute | solution.py:100
  14.6 5.2 %copy-start.62 = (s32[2]{0:T(128)S(1)}, s32[2]{0:T(128)}, u32[]{:S(2)}) copy-start(s32[2]{0:T(128)} %param.27) | copy-start | bytes 28
  14.6 7.8 %copy-start.22 = (f32[1,16,1024]{2,1,0:T(8,128)S(1)}, f32[1,16,1024]{2,1,0:T(8,128)}, u32[]{:S(2)}) copy-start(f32[1,16,1024]{2,1,0:T(8,128)} %param.17) | copy-start | bytes 196612
  14.6 7.8 %copy-start.41 = (f32[16]{0:T(128)S(1)}, f32[16]{0:T(128)}, u32[]{:S(2)}) copy-start(f32[16]{0:T(128)} %param.18) | copy-start | bytes 196
  14.6 7.8 %copy-start.42 = (f32[16]{0:T(128)S(1)}, f32[16]{0:T(128)}, u32[]{:S(2)}) copy-start(f32[16]{0:T(128)} %param.19) | copy-start | bytes 196
  15.5 71.4 %collective-permute-start.1 = (bf16[3,1024]{0,1:T(8,128)(2,1)}, bf16[3,1024]{0,1:T(8,128)(2,1)}, u32[]{:S(2)}, u32[]{:S(2)}) collective-permute-start(bf16[3,1024]{0,1:T(8,128)(2,1)} %slice_bitcast_fusion.2), channel_id=1, source_target_pairs={{0,32},{32,64},{64,96},{96,128},{128,160},{160,192},{192,224},{1,3... | collective-permute-start | bytes 18440 | tf_op jit(solution)/shard_map/ppermute | solution.py:23
  16.8 111.1 %collective-permute-start.13 = (f32[16,64,256]{2,1,0:T(8,128)}, f32[16,64,256]{2,1,0:T(8,128)}, u32[]{:S(2)}, u32[]{:S(2)}) collective-permute-start(f32[16,64,256]{2,1,0:T(8,128)} %bitcast.105), channel_id=1, source_target_pairs={{0,1},{1,0},{2,3},{3,2},{4,5},{5,4},{6,7},{7,6},{8,9},{9,8},{10,11... | collective-permute-start | bytes 3145736 | tf_op jit(solution)/shard_map/ppermute | solution.py:100
  17.4 15.3 %copy-start.33 = (f32[4,1024]{1,0:T(4,128)S(1)}, f32[4,1024]{1,0:T(4,128)}, u32[]{:S(2)}) copy-start(f32[4,1024]{1,0:T(4,128)} %param.21) | copy-start | bytes 49156
  17.4 15.3 %copy-start.63 = (u32[256]{0:T(256)S(1)}, u32[256]{0:T(256)}, u32[]{:S(2)}) copy-start(u32[256]{0:T(256)} %constant.168) | copy-start | bytes 3076
  22.4 24.3 %copy-start.11 = (bf16[1,1024,1024]{2,1,0:T(8,128)(2,1)S(1)}, bf16[1,1024,1024]{2,1,0:T(8,128)(2,1)}, u32[]{:S(2)}) copy-start(bf16[1,1024,1024]{2,1,0:T(8,128)(2,1)} %param.16) | copy-start | bytes 6291460
  25.4 5.0 %copy-start.29 = (f32[2,8,2,128]{3,1,2,0:T(8,128)}, f32[2,8,2,128]{3,1,2,0:T(8,128)S(1)}, u32[]{:S(2)}) copy-start(f32[2,8,2,128]{3,1,2,0:T(8,128)S(1)} %copy.128) | copy-start | bytes 49156
  26.1 4.4 %copy-start.31 = (f32[2,8,2,128]{3,1,2,0:T(8,128)}, f32[2,8,2,128]{3,1,2,0:T(8,128)S(1)}, u32[]{:S(2)}) copy-start(f32[2,8,2,128]{3,1,2,0:T(8,128)S(1)} %copy.127) | copy-start | bytes 49156
  26.5 7.7 %copy-start.25 = (f32[2,8,2,128]{3,1,2,0:T(8,128)}, f32[2,8,2,128]{3,1,2,0:T(8,128)S(1)}, u32[]{:S(2)}) copy-start(f32[2,8,2,128]{3,1,2,0:T(8,128)S(1)} %copy.129) | copy-start | bytes 49156
  34.1 7.3 %copy-start.60 = (f32[128]{0:T(128)}, f32[128]{0:T(128)S(1)}, u32[]{:S(2)}) copy-start(f32[128]{0:T(128)S(1)} %get-tuple-element.70) | copy-start | bytes 1540
  41.4 9.1 %copy-start.61 = (f32[128]{0:T(128)S(1)}, f32[128]{0:T(128)}, u32[]{:S(2)}) copy-start(f32[128]{0:T(128)} %copy-done.60) | copy-start | bytes 1540
  98.6 2.7 %copy-start.24 = (f32[1,3,4096]{2,0,1:T(1,128)S(1)}, f32[1,3,4096]{2,0,1:T(1,128)}, u32[]{:S(2)}) copy-start(f32[1,3,4096]{2,0,1:T(1,128)} %param.25) | copy-start | bytes 147460
  100.2 2.0 copy-start.7
  103.6 16.8 %copy-start.2 = (bf16[1024,512]{1,0:T(8,128)(2,1)}, bf16[1024,512]{1,0:T(8,128)(2,1)S(1)}, u32[]{:S(2)}) copy-start(bf16[1024,512]{1,0:T(8,128)(2,1)S(1)} %multiply_convert_fusion.9) | copy-start | bytes 3145732
  104.7 1.9 copy-start.15
  104.7 1.9 copy-start.23
  104.7 1.9 copy-start.30
  104.7 1.9 copy-start.35
  105.3 2.8 %copy-start.6 = (f32[16,64,256]{2,1,0:T(8,128)}, f32[16,64,256]{2,1,0:T(8,128)S(1)}, u32[]{:S(2)}) copy-start(f32[16,64,256]{2,1,0:T(8,128)S(1)} %fusion.69) | copy-start | bytes 3145732
  106.0 5.0 %collective-permute-start.3 = (f32[4,64,256]{2,1,0:T(8,128)S(1)}, f32[4,64,256]{2,1,0:T(8,128)S(1)}, u32[]{:S(2)}, u32[]{:S(2)}) collective-permute-start(f32[4,64,256]{2,1,0:T(8,128)S(1)} %bitcast_add_fusion.10), channel_id=1, source_target_pairs={{0,32},{1,33},{2,34},{3,35},{4,36},{5,37},{6,38},{7,39},{8,40},{9,... | collective-permute-start | bytes 786440 | tf_op jit(solution)/shard_map/ppermute | solution.py:161
  108.1 2.8 %copy-start.55 = (f32[4]{0:T(128)S(1)}, f32[4]{0:T(128)}, u32[]{:S(2)}) copy-start(f32[4]{0:T(128)} %get-tuple-element.67) | copy-start | bytes 52
  108.1 3.6 %copy-start.16 = (bf16[256,1024]{0,1:T(8,128)(2,1)S(1)}, bf16[256,1024]{0,1:T(8,128)(2,1)}, u32[]{:S(2)}) copy-start(bf16[256,1024]{0,1:T(8,128)(2,1)} %get-tuple-element.22) | copy-start | bytes 1572868
  108.2 3.6 %copy-start.28 = (f32[2,8,2,128]{3,1,2,0:T(8,128)S(1)}, f32[2,8,2,128]{3,1,2,0:T(8,128)}, u32[]{:S(2)}) copy-start(f32[2,8,2,128]{3,1,2,0:T(8,128)} %copy-done.27) | copy-start | bytes 49156
  108.2 3.6 %copy-start.36 = (f32[16,256]{1,0:T(8,128)S(1)}, f32[16,256]{1,0:T(8,128)}, u32[]{:S(2)}) copy-start(f32[16,256]{1,0:T(8,128)} %get-tuple-element.71) | copy-start | bytes 49156
  111.1 3.6 %collective-permute-start.4 = (f32[4,64,256]{2,1,0:T(8,128)S(1)}, f32[4,64,256]{2,1,0:T(8,128)S(1)}, u32[]{:S(2)}, u32[]{:S(2)}) collective-permute-start(f32[4,64,256]{2,1,0:T(8,128)S(1)} %bitcast_add_fusion.9), channel_id=1, source_target_pairs={{0,32},{32,64},{1,33},{33,65},{2,34},{34,66},{3,35},{35,67},{4,36}... | collective-permute-start | bytes 786440 | tf_op jit(solution)/shard_map/ppermute | solution.py:161
  111.8 2.9 %copy-start.54 = (f32[4]{0:T(128)S(1)}, f32[4]{0:T(128)}, u32[]{:S(2)}) copy-start(f32[4]{0:T(128)} %get-tuple-element.66) | copy-start | bytes 52
  111.8 3.6 %copy-start.14 = (bf16[256,1024]{0,1:T(8,128)(2,1)S(1)}, bf16[256,1024]{0,1:T(8,128)(2,1)}, u32[]{:S(2)}) copy-start(bf16[256,1024]{0,1:T(8,128)(2,1)} %get-tuple-element.21) | copy-start | bytes 1572868
  111.8 3.6 %copy-start.26 = (f32[2,8,2,128]{3,1,2,0:T(8,128)S(1)}, f32[2,8,2,128]{3,1,2,0:T(8,128)}, u32[]{:S(2)}) copy-start(f32[2,8,2,128]{3,1,2,0:T(8,128)} %copy-done.25) | copy-start | bytes 49156
  111.8 3.6 %copy-start.34 = (f32[16,256]{1,0:T(8,128)S(1)}, f32[16,256]{1,0:T(8,128)}, u32[]{:S(2)}) copy-start(f32[16,256]{1,0:T(8,128)} %get-tuple-element.74) | copy-start | bytes 49156
  114.7 2.1 collective-permute-start.5
  115.5 2.2 copy-start.40
  115.5 2.2 copy-start.45
  116.9 2.6 copy-start.52
  116.9 5.9 %copy-start.51 = (f32[4]{0:T(128)S(1)}, f32[4]{0:T(128)}, u32[]{:S(2)}) copy-start(f32[4]{0:T(128)} %get-tuple-element.63) | copy-start | bytes 52
  117.0 2.4 collective-permute-start.6
  117.7 8.1 %copy-start.49 = (f32[4]{0:T(128)S(1)}, f32[4]{0:T(128)}, u32[]{:S(2)}) copy-start(f32[4]{0:T(128)} %get-tuple-element.62) | copy-start | bytes 52
  119.5 3.3 %collective-permute-start.7 = (f32[4,64,256]{2,1,0:T(8,128)S(1)}, f32[4,64,256]{2,1,0:T(8,128)S(1)}, u32[]{:S(2)}, u32[]{:S(2)}) collective-permute-start(f32[4,64,256]{2,1,0:T(8,128)S(1)} %bitcast_add_fusion.6), channel_id=1, source_target_pairs={{32,64},{64,96},{96,128},{128,160},{33,65},{65,97},{97,129},{129,1... | collective-permute-start | bytes 786440 | tf_op jit(solution)/shard_map/ppermute | solution.py:161
  122.1 47.8 %copy-start.48 = (f32[4]{0:T(128)S(1)}, f32[4]{0:T(128)}, u32[]{:S(2)}) copy-start(f32[4]{0:T(128)} %get-tuple-element.61) | copy-start | bytes 52
  122.8 57.2 %copy-start.47 = (f32[4]{0:T(128)S(1)}, f32[4]{0:T(128)}, u32[]{:S(2)}) copy-start(f32[4]{0:T(128)} %get-tuple-element.60) | copy-start | bytes 52
  122.9 2.1 collective-permute-start.8
  125.8 65.1 %copy-start.46 = (f32[4]{0:T(128)S(1)}, f32[4]{0:T(128)}, u32[]{:S(2)}) copy-start(f32[4]{0:T(128)} %get-tuple-element.59) | copy-start | bytes 52
  126.6 43.3 %collective-permute-start.9 = (f32[4,64,256]{2,1,0:T(8,128)}, f32[4,64,256]{2,1,0:T(8,128)}, u32[]{:S(2)}, u32[]{:S(2)}) collective-permute-start(f32[4,64,256]{2,1,0:T(8,128)} %bitcast_add_fusion.4), channel_id=1, source_target_pairs={{96,128},{128,160},{160,192},{192,224},{97,129},{129,161},{161,193... | collective-permute-start | bytes 786440 | tf_op jit(solution)/shard_map/ppermute | solution.py:161
  130.3 116.6 %copy-start.44 = (f32[16]{0:T(128)S(1)}, f32[16]{0:T(128)}, u32[]{:S(2)}) copy-start(f32[16]{0:T(128)} %copy-done.43) | copy-start | bytes 196
  130.3 116.6 %copy-start.50 = (f32[16]{0:T(128)S(1)}, f32[16]{0:T(128)}, u32[]{:S(2)}) copy-start(f32[16]{0:T(128)} %select_reduce_fusion) | copy-start | bytes 196
  130.3 116.6 %copy-start.56 = (f32[16]{0:T(128)S(1)}, f32[16]{0:T(128)}, u32[]{:S(2)}) copy-start(f32[16]{0:T(128)} %get-tuple-element.79) | copy-start | bytes 196
  130.3 116.6 %copy-start.57 = (f32[16]{0:T(128)S(1)}, f32[16]{0:T(128)}, u32[]{:S(2)}) copy-start(f32[16]{0:T(128)} %get-tuple-element.80) | copy-start | bytes 196
  130.3 116.6 %copy-start.59 = (f32[16]{0:T(128)S(1)}, f32[16]{0:T(128)}, u32[]{:S(2)}) copy-start(f32[16]{0:T(128)} %negate_exponential_fusion.3) | copy-start | bytes 196
  170.9 9.0 %collective-permute-start.10 = (f32[4,64,256]{2,1,0:T(8,128)S(1)}, f32[4,64,256]{2,1,0:T(8,128)S(1)}, u32[]{:S(2)}, u32[]{:S(2)}) collective-permute-start(f32[4,64,256]{2,1,0:T(8,128)S(1)} %bitcast_add_fusion.3), channel_id=1, source_target_pairs={{128,160},{160,192},{192,224},{129,161},{161,193},{193,225},{130,1... | collective-permute-start | bytes 786440 | tf_op jit(solution)/shard_map/ppermute | solution.py:161
  180.1 10.8 %collective-permute-start.11 = (f32[4,64,256]{2,1,0:T(8,128)S(1)}, f32[4,64,256]{2,1,0:T(8,128)S(1)}, u32[]{:S(2)}, u32[]{:S(2)}) collective-permute-start(f32[4,64,256]{2,1,0:T(8,128)S(1)} %bitcast_add_fusion.2), channel_id=1, source_target_pairs={{160,192},{192,224},{161,193},{193,225},{162,194},{194,226},{163,1... | collective-permute-start | bytes 786440 | tf_op jit(solution)/shard_map/ppermute | solution.py:161
  191.0 55.9 %copy-start.5 = (f32[16,64,256]{2,1,0:T(8,128)S(1)}, f32[16,64,256]{2,1,0:T(8,128)}, u32[]{:S(2)}) copy-start(f32[16,64,256]{2,1,0:T(8,128)} %copy-done.4) | copy-start | bytes 3145732
  191.0 11.7 %collective-permute-start.12 = (f32[4,64,256]{2,1,0:T(8,128)S(1)}, f32[4,64,256]{2,1,0:T(8,128)S(1)}, u32[]{:S(2)}, u32[]{:S(2)}) collective-permute-start(f32[4,64,256]{2,1,0:T(8,128)S(1)} %bitcast_add_fusion.1), channel_id=1, source_target_pairs={{192,224},{193,225},{194,226},{195,227},{196,228},{197,229},{198,2... | collective-permute-start | bytes 786440 | tf_op jit(solution)/shard_map/ppermute | solution.py:161
  246.9 3.6 %copy-start.3 = (bf16[1024,512]{1,0:T(8,128)(2,1)S(1)}, bf16[1024,512]{1,0:T(8,128)(2,1)}, u32[]{:S(2)}) copy-start(bf16[1024,512]{1,0:T(8,128)(2,1)} %copy-done.2) | copy-start | bytes 3145732
  250.5 1.9 copy-start.20
  250.5 2.6 copy-start.17
  250.5 2.6 copy-start.21
  252.4 2.2 copy-start.10
  254.5 4.5 %copy-start.1 = (s32[2,1]{0,1:T(1,128)S(1)}, s32[2,1]{0,1:T(1,128)}, u32[]{:S(2)}) copy-start(s32[2,1]{0,1:T(1,128)} %param.26) | copy-start | bytes 28
  (15 other events, 20.2 us)
Sparse Core Ops, SparseCore 0:
  130.4 116.4 all-reduce.3

commit v2 on v1

--- a/solution.py
+++ b/solution.py
@@ -97,14 +97,17 @@
     on_chip = (want // n_req) == ctx_pos
     pick = want % n_req
     swap = [(src, n_req - 1 - src) for src in range(n_req)]
-    other_pool, other_conv = lax.ppermute((ssm_pool[0], conv_pool[0]), "req", swap)
-    mine = pick == req_pos
-    first_conv = lax.psum(
-        jnp.where(on_chip, jnp.where(mine, conv_pool[0], other_conv), 0.0), "ctx"
-    )
-    first_state = lax.psum(
-        jnp.where(on_chip, jnp.where(mine, ssm_pool[0], other_pool), 0.0), "ctx"
-    )
+    other_pool = lax.ppermute(ssm_pool[0], "req", swap)
+    state_pick = jnp.where(
+        on_chip, jnp.where(pick == req_pos, ssm_pool[0], other_pool), 0.0
+    )
+    state_pick, x_in = lax.optimization_barrier((state_pick, x_in))
+    first_state = lax.psum(state_pick, "ctx")
+    slot_pos = ctx_pos * n_req + req_pos
+    conv_picks = jnp.stack(
+        [jnp.where(owner[r, 0] == slot_pos, conv_pool[0], 0.0) for r in range(n_req)]
+    )
+    first_conv = lax.psum(conv_picks, ("ctx", "req"))[req_pos]
 
     tail_x = x_in[0, tokens - (K - 1) :, :]
     tail_bc = bc_in[0, tokens - (K - 1) :, :]

time: 271 us -> 270 us (level); the launches traced: 266 us -> 269 us
  blocking collectives: 36.4 us -> 63.2 us
  waiting for transfers between devices: 101 us -> 84.7 us
  local copies, waits for them, and re-layouts: 33.5 us -> 26 us
  other arithmetic: 47 us -> 43.6 us
  matrix products: 16.5 us -> 19.6 us
    psum x1, waiting for transfers between devices: 41.1 us -> 0.01 us  [on_device(): first_state = lax.psum(state_pick, 'ctx')]
    ppermute x10, waiting for transfers between devices: 59.9 us -> 80 us  [on_device(): got = lax.ppermute(sent, 'ctx', pairs)]
    unnamed x0 -> x1, blocking collectives: none -> 19 us
    unnamed x151 -> x143, local copies, waits for them, and re-layouts: 23.4 us -> 9.74 us
    psum x1, blocking collectives: 36.4 us -> 44.2 us  [on_device(): first_conv = lax.psum(conv_picks, ('ctx', 'req'))[req_pos]]
    ppermute x2, waiting for transfers between devices: 0.01 us -> 4.73 us  [passed_along(): lax.ppermute(value, axis, [(source, source + steps) for source in range(i...]
    dot_general x4, matrix products: 0.85 us -> 3.71 us  [block_output(): jnp.einsum('qgn,sgn->gqs', c_blk, b_blk, preferred_element_type=jnp.float32)]
    optimization_barrier x0 -> x1, local copies, waits for them, and re-layouts: none -> 2.85 us  [on_device(): state_pick, x_in = lax.optimization_barrier((state_pick, x_in))]
  transfers between devices with their start and end apart: 15 -> 14, of which waited for: 5 -> 5; matrix products, arithmetic and copies ran while one was open for 31% -> 26% of each run, Pallas kernels for 0% -> 0%
where the time goes in v2:
time: 270 us; the launch traced here: 269 us
  waiting for transfers between devices  84.7 us (31%)
  blocking collectives  63.2 us (23%)
  other arithmetic  43.6 us (16%)
  local copies, waits for them, and re-layouts  26 us (10%)
  between operations  20 us (7%)
  matrix products  19.6 us (7%)
  starting transfers between devices  12.3 us (5%)
    ppermute x10, waiting for transfers between devices, on_device(): got = lax.ppermute(sent, 'ctx', pairs)  80 us
    psum x1, blocking collectives, on_device(): first_conv = lax.psum(conv_picks, ('ctx', 'req'))[req_pos]  44.2 us
    unnamed x1, blocking collectives  19 us
    convert_element_type x2, other arithmetic, causal_conv(): return jax.nn.silu(total).astype(jnp.bfloat16)  11.8 us
    unnamed x143, local copies, waits for them, and re-layouts  9.74 us
    ppermute x10, starting transfers between devices, on_device(): got = lax.ppermute(sent, 'ctx', pairs)  9.63 us
    dot_general x4, matrix products, block_output(): jnp.einsum('hqs,shp->qhp', weights, x_blk, preferred_element_type=jnp.flo...  7.92 us
    another operation x5, other arithmetic  6.93 us
  transfers between devices with their start and end apart: 14, of which 5 were waited for; matrix products, arithmetic and copies ran while one was open for 26% of the time, Pallas kernels for 0%

profile of v2, /device:TPU:246, one launch (start us, length us, event | category | flops | bytes accessed | tf_op | source)
XLA Modules:
  0.0 269.5 jit_solution(793136858071157633)
XLA Ops:
  7.4 0.9 slice_bitcast_fusion.3
  8.2 1.3 collective-permute-start.2
  9.5 0.7 iota_compare_fusion
  10.2 1.2 dynamic_slice.106
  12.8 0.7 fusion.110
  13.4 1.4 fusion.137
  16.1 0.7 broadcast_select_fusion.1
  16.9 44.2 %psum.14 = f32[2,3,1024]{2,0,1:T(2,128)S(1)} all-reduce(f32[2,3,1024]{2,0,1:T(2,128)S(1)} %pad_maximum_fusion.2), channel_id=1, replica_groups=mesh['ctx'=8,'head'=16,'req'=2] {'ctx','req'}, use_global_device_ids=true, to_apply=%region_0.1 | all-reduce | flops 6144 | bytes 49152 | tf_op jit(solution)/shard_map/psum | solution.py:110
  61.1 1.5 fusion.136
  62.6 1.3 dynamic-slice_bitcast_fusion.1
  63.9 0.7 constant_dynamic-slice_fusion.13
  64.6 0.9 squeeze.141
  65.4 0.8 fusion.132
  66.4 2.3 reduce-window.14
  71.5 0.7 exponential_bitcast_fusion.2
  73.4 0.7 exponential_bitcast_fusion
  76.2 19.0 %all-reduce = f32[128]{0:T(128)S(1)} all-reduce(f32[128]{0:T(128)S(1)} %get-tuple-element.73), channel_id=2, replica_groups=mesh['ctx'=8,'head'=16,'req'=2] {'ctx'}, use_global_device_ids=true, to_apply=%add | all-reduce | flops 128 | bytes 1024
  95.4 4.5 %reduce-window.16 = f32[16,8,128]{2,1,0:T(8,128)S(1)} reduce-window(f32[16,8,128]{2,1,0:T(8,128)S(1)} %fusion.106, f32[]{:T(128)} %constant.138.clone.1), window={size=1x1x128 pad=0_0x0_0x127_0}, to_apply=%region_6.7 | reduce-window | flops 2080768 | bytes 131076 | tf_op jit(solution)/shard_map/reduce-window.2
  104.6 1.0 copy.66
  105.6 0.7 exp.159
  106.3 0.7 exp.161
  107.0 0.7 exp.163
  107.6 0.7 mul.627
  108.3 3.9 %copy.78 = bf16[1,1024,1024]{1,2,0:T(8,128)(2,1)} copy(bf16[1,1024,1024]{2,1,0:T(8,128)(2,1)} %param.16) | data formatting | bytes 4194304 | tf_op args[2]
  112.6 1.2 multiply_convert_fusion.9
  113.8 0.9 fusion.92
  114.8 0.9 fusion.87
  115.7 0.9 fusion.97
  116.6 0.9 fusion.82
  117.6 2.4 select_select_fusion
  119.9 2.9 %copy.67 = bf16[1,1024,1024]{1,2,0:T(8,128)(2,1)S(1)} copy(bf16[1,1024,1024]{2,1,0:T(8,128)(2,1)} %param.14) | data formatting | bytes 4194304 | tf_op jit(solution)/shard_map/optimization_barrier | solution.py:104
  122.8 0.9 slice_bitcast_fusion.2
  123.7 1.3 collective-permute-start.1
  124.9 2.4 bitcast_convert_fusion
  127.4 4.7 %collective-permute-done.1 = bf16[3,1024]{0,1:T(8,128)(2,1)S(1)} collective-permute-done((bf16[3,1024]{0,1:T(8,128)(2,1)}, bf16[3,1024]{0,1:T(8,128)(2,1)S(1)}, u32[]{:S(2)}, u32[]{:S(2)}) %collective-permute-start.1) | collective-permute-done | bytes 6176 | tf_op jit(solution)/shard_map/ppermute | solution.py:23
  132.1 1.1 bitcast_select_fusion
  133.2 10.6 %multiply_convert_fusion.4 = bf16[1024,1024]{0,1:T(8,128)(2,1)S(1)} fusion(f32[1024,1024]{0,1:T(8,128)} %bitcast_convert_fusion, f32[3,1024]{0,1:T(8,128)S(1)} %bitcast_select_fusion, f32[1024]{0:T(1024)} %bitcast.372, f32[1024]{0:T(1024)} %bitcast.373, f32[1024]{0:T(1024)} %bitcast.371, f32[1024]{0:T(1024)} %bitcast.370), kind=kLoop, calls=%fused_computation.26 | loop fusion | flops 15728640 | bytes 6320128 | tf_op jit(solution)/shard_map/convert_element_type | solution.py:32
  146.6 0.9 collective-permute-start.3
  147.5 1.4 fusion.47
  149.0 0.7 collective-permute-start.4
  149.8 2.6 fusion.46
  152.5 0.7 collective-permute-start.5
  153.2 1.4 fusion.48
  154.7 0.7 collective-permute-start.6
  155.5 2.5 fusion.45
  158.2 0.7 collective-permute-start.7
  158.9 1.7 fusion.58
  160.7 0.7 collective-permute-start.8
  161.4 1.6 fusion.57
  163.2 1.3 collective-permute-start.9
  164.6 58.0 %collective-permute-done.9 = f32[4,64,256]{2,1,0:T(8,128)S(1)} collective-permute-done((f32[4,64,256]{2,1,0:T(8,128)S(1)}, f32[4,64,256]{2,1,0:T(8,128)S(1)}, u32[]{:S(2)}, u32[]{:S(2)}) %collective-permute-start.9) | collective-permute-done | bytes 262176 | tf_op jit(solution)/shard_map/ppermute | solution.py:164
  222.7 1.3 collective-permute-start.10
  224.0 8.4 %collective-permute-done.10 = f32[4,64,256]{2,1,0:T(8,128)S(1)} collective-permute-done((f32[4,64,256]{2,1,0:T(8,128)S(1)}, f32[4,64,256]{2,1,0:T(8,128)S(1)}, u32[]{:S(2)}, u32[]{:S(2)}) %collective-permute-start.10) | collective-permute-done | bytes 262176 | tf_op jit(solution)/shard_map/ppermute | solution.py:164
  232.5 1.3 collective-permute-start.11
  233.8 6.9 %collective-permute-done.11 = f32[4,64,256]{2,1,0:T(8,128)S(1)} collective-permute-done((f32[4,64,256]{2,1,0:T(8,128)S(1)}, f32[4,64,256]{2,1,0:T(8,128)S(1)}, u32[]{:S(2)}, u32[]{:S(2)}) %collective-permute-start.11) | collective-permute-done | bytes 262176 | tf_op jit(solution)/shard_map/ppermute | solution.py:164
  240.9 1.5 collective-permute-start.12
  242.4 6.7 %collective-permute-done.12 = f32[4,64,256]{2,1,0:T(8,128)S(1)} collective-permute-done((f32[4,64,256]{2,1,0:T(8,128)S(1)}, f32[4,64,256]{2,1,0:T(8,128)S(1)}, u32[]{:S(2)}, u32[]{:S(2)}) %collective-permute-start.12) | collective-permute-done | bytes 262176 | tf_op jit(solution)/shard_map/ppermute | solution.py:164
  249.1 1.1 dynamic-slice_select_fusion
  250.3 3.7 %add_bitcast_fusion = (f32[1,1,16,64,256]{4,3,2,1,0:T(8,128)}, f32[16,64,256]{2,1,0:T(8,128)S(1)}, f32[16,64,256]{2,1,0:T(8,128)S(1)}) fusion(f32[16,64,256]{2,1,0:T(8,128)} %copy-done.1, f32[16]{0:T(128)S(1)} %copy-done.57, f32[16]{0:T(128)S(1)} %copy-done.44, f32[16,64,256]{2,1,0:T(8,128)S(1)} %fusion.72, f32[16]{0:T(128)S(1)} %copy-done.45, ...), kind=kLoop, calls=%fused_computation.95 | loop fusion | flops 2883584 | bytes 9437568 | tf_op jit(solution)/shard_map/broadcast_in_dim | solution.py:200
  254.0 1.9 fusion.66
  256.0 0.7 fusion.59
  256.7 0.8 fusion.60
  258.1 1.9 fusion.13
  260.1 2.6 copy.79
  (214 shorter events, 13.7 us)
Async XLA Ops:
  7.2 67.1 %copy-start.60 = (u32[256]{0:T(256)S(1)}, u32[256]{0:T(256)}, u32[]{:S(2)}) copy-start(u32[256]{0:T(256)} %constant.168) | copy-start | bytes 3076
  7.2 66.9 %copy-start.12 = (f32[1,16,1024]{2,1,0:T(8,128)S(1)}, f32[1,16,1024]{2,1,0:T(8,128)}, u32[]{:S(2)}) copy-start(f32[1,16,1024]{2,1,0:T(8,128)} %param.17) | copy-start | bytes 196612
  7.2 66.9 %copy-start.41 = (f32[16]{0:T(128)S(1)}, f32[16]{0:T(128)}, u32[]{:S(2)}) copy-start(f32[16]{0:T(128)} %param.18) | copy-start | bytes 196
  7.2 66.9 %copy-start.42 = (f32[16]{0:T(128)S(1)}, f32[16]{0:T(128)}, u32[]{:S(2)}) copy-start(f32[16]{0:T(128)} %param.19) | copy-start | bytes 196
  7.2 243.1 %all-reduce.3.cloned.1.call-start = ((), (), s32[]{:S(2)}) async-start(), calls=%async_computation | async-start | bytes 2097152 | tf_op jit(solution)/shard_map/psum | solution.py:105
  7.3 110.3 %collective-permute-start = (f32[16,64,256]{2,1,0:T(8,128)}, f32[16,64,256]{2,1,0:T(8,128)}, u32[]{:S(2)}, u32[]{:S(2)}) collective-permute-start(f32[16,64,256]{2,1,0:T(8,128)} %bitcast.349), channel_id=1, source_target_pairs={{0,1},{1,0},{2,3},{3,2},{4,5},{5,4},{6,7},{7,6},{8,9},{9,8},{10,11... | collective-permute-start | bytes 3145736 | tf_op jit(solution)/shard_map/ppermute | solution.py:100
  8.2 104.1 %collective-permute-start.2 = (bf16[3,4096]{1,0:T(4,128)(2,1)S(1)}, bf16[3,4096]{1,0:T(4,128)(2,1)S(1)}, u32[]{:S(2)}, u32[]{:S(2)}) collective-permute-start(bf16[3,4096]{1,0:T(4,128)(2,1)S(1)} %slice_bitcast_fusion.3), channel_id=1, source_target_pairs={{0,32},{32,64},{64,96},{96,128},{128,160},{160,192},{192,224},{1,3... | collective-permute-start | bytes 73736 | tf_op jit(solution)/shard_map/ppermute | solution.py:23
  12.7 88.0 %copy-start.22 = (f32[1024]{0:T(1024)}, f32[1024]{0:T(1024)S(1)}, u32[]{:S(2)}) copy-start(f32[1024]{0:T(1024)S(1)} %fusion.111) | copy-start | bytes 12292
  69.1 31.3 %copy-start.30 = (f32[2,8,2,128]{3,1,2,0:T(8,128)}, f32[2,8,2,128]{3,1,2,0:T(8,128)S(1)}, u32[]{:S(2)}) copy-start(f32[2,8,2,128]{3,1,2,0:T(8,128)S(1)} %copy.128) | copy-start | bytes 49156
  69.7 30.7 %copy-start.28 = (f32[2,8,2,128]{3,1,2,0:T(8,128)}, f32[2,8,2,128]{3,1,2,0:T(8,128)S(1)}, u32[]{:S(2)}) copy-start(f32[2,8,2,128]{3,1,2,0:T(8,128)S(1)} %copy.127) | copy-start | bytes 49156
  70.2 25.2 %copy-start.26 = (f32[2,8,2,128]{3,1,2,0:T(8,128)}, f32[2,8,2,128]{3,1,2,0:T(8,128)S(1)}, u32[]{:S(2)}) copy-start(f32[2,8,2,128]{3,1,2,0:T(8,128)S(1)} %copy.129) | copy-start | bytes 49156
  76.1 24.0 %copy-start.43 = (f32[16]{0:T(128)}, f32[16]{0:T(128)S(1)}, u32[]{:S(2)}) copy-start(f32[16]{0:T(128)S(1)} %get-tuple-element.74) | copy-start | bytes 196
  100.0 12.2 %copy-start.21 = (f32[1,3,4096]{2,0,1:T(1,128)S(1)}, f32[1,3,4096]{2,0,1:T(1,128)}, u32[]{:S(2)}) copy-start(f32[1,3,4096]{2,0,1:T(1,128)} %param.25) | copy-start | bytes 147460
  112.6 4.9 %copy-start.9 = (f32[1,16,64,256]{3,2,1,0:T(8,128)S(1)}, f32[1,16,64,256]{3,2,1,0:T(8,128)}, u32[]{:S(2)}) copy-start(f32[1,16,64,256]{3,2,1,0:T(8,128)} %param.23) | copy-start | bytes 3145732
  123.7 8.5 %collective-permute-start.1 = (bf16[3,1024]{0,1:T(8,128)(2,1)}, bf16[3,1024]{0,1:T(8,128)(2,1)S(1)}, u32[]{:S(2)}, u32[]{:S(2)}) collective-permute-start(bf16[3,1024]{0,1:T(8,128)(2,1)} %slice_bitcast_fusion.2), channel_id=1, source_target_pairs={{0,32},{32,64},{64,96},{96,128},{128,160},{160,192},{192,224},{1,3... | collective-permute-start | bytes 18440 | tf_op jit(solution)/shard_map/ppermute | solution.py:23
  133.2 10.8 %copy-start.17 = (f32[256,16]{0,1:T(8,128)S(1)}, f32[256,16]{0,1:T(8,128)}, u32[]{:S(2)}) copy-start(f32[256,16]{0,1:T(8,128)} %get-tuple-element.84) | copy-start | bytes 49156
  133.2 10.8 %copy-start.18 = (f32[256,16]{0,1:T(8,128)S(1)}, f32[256,16]{0,1:T(8,128)}, u32[]{:S(2)}) copy-start(f32[256,16]{0,1:T(8,128)} %get-tuple-element.52) | copy-start | bytes 49156
  133.2 10.8 %copy-start.19 = (f32[256,16]{0,1:T(8,128)S(1)}, f32[256,16]{0,1:T(8,128)}, u32[]{:S(2)}) copy-start(f32[256,16]{0,1:T(8,128)} %get-tuple-element.82) | copy-start | bytes 49156
  144.0 5.7 %copy-start.5 = (bf16[256,1024]{0,1:T(8,128)(2,1)}, bf16[256,1024]{0,1:T(8,128)(2,1)S(1)}, u32[]{:S(2)}) copy-start(bf16[256,1024]{0,1:T(8,128)(2,1)S(1)} %get-tuple-element.25) | copy-start | bytes 1572868
  144.0 11.4 %copy-start.7 = (bf16[256,1024]{0,1:T(8,128)(2,1)}, bf16[256,1024]{0,1:T(8,128)(2,1)S(1)}, u32[]{:S(2)}) copy-start(bf16[256,1024]{0,1:T(8,128)(2,1)S(1)} %get-tuple-element.24) | copy-start | bytes 1572868
  145.3 2.1 copy-start.16
  145.3 2.1 copy-start.20
  145.3 2.1 copy-start.31
  145.3 2.1 copy-start.34
  145.9 3.0 %copy-start.1 = (f32[16,64,256]{2,1,0:T(8,128)}, f32[16,64,256]{2,1,0:T(8,128)S(1)}, u32[]{:S(2)}) copy-start(f32[16,64,256]{2,1,0:T(8,128)S(1)} %fusion.69) | copy-start | bytes 3145732
  146.6 2.3 collective-permute-start.3
  147.5 2.3 copy-start.15
  147.5 2.3 copy-start.29
  147.5 2.3 copy-start.35
  149.0 3.4 %collective-permute-start.4 = (f32[4,64,256]{2,1,0:T(8,128)S(1)}, f32[4,64,256]{2,1,0:T(8,128)S(1)}, u32[]{:S(2)}, u32[]{:S(2)}) collective-permute-start(f32[4,64,256]{2,1,0:T(8,128)S(1)} %bitcast_add_fusion.9), channel_id=1, source_target_pairs={{0,32},{32,64},{1,33},{33,65},{2,34},{34,66},{3,35},{35,67},{4,36}... | collective-permute-start | bytes 786440 | tf_op jit(solution)/shard_map/ppermute | solution.py:164
  149.7 2.6 copy-start.55
  149.8 3.4 %copy-start.14 = (f32[256,256]{1,0:T(8,128)S(1)}, f32[256,256]{1,0:T(8,128)}, u32[]{:S(2)}) copy-start(f32[256,256]{1,0:T(8,128)} %fusion.97) | copy-start | bytes 786436
  149.8 3.4 %copy-start.27 = (f32[2,8,2,128]{3,1,2,0:T(8,128)S(1)}, f32[2,8,2,128]{3,1,2,0:T(8,128)}, u32[]{:S(2)}) copy-start(f32[2,8,2,128]{3,1,2,0:T(8,128)} %copy-done.26) | copy-start | bytes 49156
  149.8 3.4 %copy-start.32 = (f32[16,256]{1,0:T(8,128)S(1)}, f32[16,256]{1,0:T(8,128)}, u32[]{:S(2)}) copy-start(f32[16,256]{1,0:T(8,128)} %get-tuple-element.81) | copy-start | bytes 49156
  152.5 2.2 collective-permute-start.5
  153.2 2.2 copy-start.13
  153.2 2.2 copy-start.25
  153.2 2.2 copy-start.33
  154.7 3.3 %collective-permute-start.6 = (f32[4,64,256]{2,1,0:T(8,128)S(1)}, f32[4,64,256]{2,1,0:T(8,128)S(1)}, u32[]{:S(2)}, u32[]{:S(2)}) collective-permute-start(f32[4,64,256]{2,1,0:T(8,128)S(1)} %bitcast_add_fusion.7), channel_id=1, source_target_pairs={{0,32},{32,64},{64,96},{96,128},{1,33},{33,65},{65,97},{97,129},{2... | collective-permute-start | bytes 786440 | tf_op jit(solution)/shard_map/ppermute | solution.py:164
  155.5 2.6 copy-start.53
  155.5 3.4 %copy-start.40 = (f32[16]{0:T(128)S(1)}, f32[16]{0:T(128)}, u32[]{:S(2)}) copy-start(f32[16]{0:T(128)} %param.20) | copy-start | bytes 196
  155.5 3.4 %copy-start.46 = (f32[16]{0:T(128)S(1)}, f32[16]{0:T(128)}, u32[]{:S(2)}) copy-start(f32[16]{0:T(128)} %exponential_multiply_fusion) | copy-start | bytes 196
  158.1 2.6 copy-start.52
  158.1 5.0 %copy-start.51 = (f32[4]{0:T(128)S(1)}, f32[4]{0:T(128)}, u32[]{:S(2)}) copy-start(f32[4]{0:T(128)} %get-tuple-element.66) | copy-start | bytes 52
  158.2 2.4 collective-permute-start.7
  158.9 63.7 %copy-start.50 = (f32[4]{0:T(128)S(1)}, f32[4]{0:T(128)}, u32[]{:S(2)}) copy-start(f32[4]{0:T(128)} %get-tuple-element.65) | copy-start | bytes 52
  160.6 71.8 %copy-start.49 = (f32[4]{0:T(128)S(1)}, f32[4]{0:T(128)}, u32[]{:S(2)}) copy-start(f32[4]{0:T(128)} %get-tuple-element.64) | copy-start | bytes 52
  160.7 2.3 collective-permute-start.8
  161.4 79.4 %copy-start.48 = (f32[4]{0:T(128)S(1)}, f32[4]{0:T(128)}, u32[]{:S(2)}) copy-start(f32[4]{0:T(128)} %get-tuple-element.63) | copy-start | bytes 52
  163.2 59.4 %collective-permute-start.9 = (f32[4,64,256]{2,1,0:T(8,128)S(1)}, f32[4,64,256]{2,1,0:T(8,128)S(1)}, u32[]{:S(2)}, u32[]{:S(2)}) collective-permute-start(f32[4,64,256]{2,1,0:T(8,128)S(1)} %bitcast_add_fusion.4), channel_id=1, source_target_pairs={{96,128},{128,160},{160,192},{192,224},{97,129},{129,161},{161,193... | collective-permute-start | bytes 786440 | tf_op jit(solution)/shard_map/ppermute | solution.py:164
  164.5 85.8 %copy-start.44 = (f32[16]{0:T(128)S(1)}, f32[16]{0:T(128)}, u32[]{:S(2)}) copy-start(f32[16]{0:T(128)} %copy-done.43) | copy-start | bytes 196
  164.5 85.7 %copy-start.45 = (f32[16]{0:T(128)S(1)}, f32[16]{0:T(128)}, u32[]{:S(2)}) copy-start(f32[16]{0:T(128)} %get-tuple-element.88) | copy-start | bytes 196
  164.6 85.7 %copy-start.47 = (f32[16]{0:T(128)S(1)}, f32[16]{0:T(128)}, u32[]{:S(2)}) copy-start(f32[16]{0:T(128)} %select_reduce_fusion) | copy-start | bytes 196
  164.6 85.7 %copy-start.57 = (f32[16]{0:T(128)S(1)}, f32[16]{0:T(128)}, u32[]{:S(2)}) copy-start(f32[16]{0:T(128)} %get-tuple-element.86) | copy-start | bytes 196
  164.6 85.7 %copy-start.58 = (f32[16]{0:T(128)S(1)}, f32[16]{0:T(128)}, u32[]{:S(2)}) copy-start(f32[16]{0:T(128)} %get-tuple-element.87) | copy-start | bytes 196
  222.7 9.7 %collective-permute-start.10 = (f32[4,64,256]{2,1,0:T(8,128)S(1)}, f32[4,64,256]{2,1,0:T(8,128)S(1)}, u32[]{:S(2)}, u32[]{:S(2)}) collective-permute-start(f32[4,64,256]{2,1,0:T(8,128)S(1)} %bitcast_add_fusion.3), channel_id=1, source_target_pairs={{128,160},{160,192},{192,224},{129,161},{161,193},{193,225},{130,1... | collective-permute-start | bytes 786440 | tf_op jit(solution)/shard_map/ppermute | solution.py:164
  232.5 8.3 %collective-permute-start.11 = (f32[4,64,256]{2,1,0:T(8,128)S(1)}, f32[4,64,256]{2,1,0:T(8,128)S(1)}, u32[]{:S(2)}, u32[]{:S(2)}) collective-permute-start(f32[4,64,256]{2,1,0:T(8,128)S(1)} %bitcast_add_fusion.2), channel_id=1, source_target_pairs={{160,192},{192,224},{161,193},{193,225},{162,194},{194,226},{163,1... | collective-permute-start | bytes 786440 | tf_op jit(solution)/shard_map/ppermute | solution.py:164
  240.9 8.3 %collective-permute-start.12 = (f32[4,64,256]{2,1,0:T(8,128)S(1)}, f32[4,64,256]{2,1,0:T(8,128)S(1)}, u32[]{:S(2)}, u32[]{:S(2)}) collective-permute-start(f32[4,64,256]{2,1,0:T(8,128)S(1)} %bitcast_add_fusion.1), channel_id=1, source_target_pairs={{192,224},{193,225},{194,226},{195,227},{196,228},{197,229},{198,2... | collective-permute-start | bytes 786440 | tf_op jit(solution)/shard_map/ppermute | solution.py:164
  254.0 1.9 copy-start.6
  254.0 1.9 copy-start.10
  254.0 2.7 %copy-start.8 = (bf16[256,1024]{0,1:T(8,128)(2,1)S(1)}, bf16[256,1024]{0,1:T(8,128)(2,1)}, u32[]{:S(2)}) copy-start(bf16[256,1024]{0,1:T(8,128)(2,1)} %copy-done.7) | copy-start | bytes 1572868
  254.0 2.7 %copy-start.11 = (f32[256,16,64]{0,2,1:T(8,128)S(1)}, f32[256,16,64]{0,2,1:T(8,128)}, u32[]{:S(2)}) copy-start(f32[256,16,64]{0,2,1:T(8,128)} %fusion.45) | copy-start | bytes 3145732
  256.0 2.2 copy-start.4
  256.0 2.1 copy-start.23
  (11 other events, 14.6 us)
Sparse Core Ops, SparseCore 0:
  127.5 78.3 all-reduce.2

commit v3 on v1

--- a/solution.py
+++ b/solution.py
@@ -95,16 +95,16 @@
 
     want = owner[req_pos, 0]
     on_chip = (want // n_req) == ctx_pos
-    pick = want % n_req
+    mine = (want % n_req) == req_pos
     swap = [(src, n_req - 1 - src) for src in range(n_req)]
     other_pool, other_conv = lax.ppermute((ssm_pool[0], conv_pool[0]), "req", swap)
-    mine = pick == req_pos
-    first_conv = lax.psum(
-        jnp.where(on_chip, jnp.where(mine, conv_pool[0], other_conv), 0.0), "ctx"
-    )
-    first_state = lax.psum(
-        jnp.where(on_chip, jnp.where(mine, ssm_pool[0], other_pool), 0.0), "ctx"
-    )
+    state_pick = jnp.where(on_chip, jnp.where(mine, ssm_pool[0], other_pool), 0.0)
+    conv_pick = jnp.where(on_chip, jnp.where(mine, conv_pool[0], other_conv), 0.0)
+    picked = jnp.concatenate([state_pick.reshape(-1), conv_pick.reshape(-1)])
+    picked, x_in, bc_in, dt_raw = lax.optimization_barrier((picked, x_in, bc_in, dt_raw))
+    picked = lax.psum(picked, "ctx")
+    first_state = picked[: state_pick.size].reshape(state_pick.shape)
+    first_conv = picked[state_pick.size :].reshape(conv_pick.shape)
 
     tail_x = x_in[0, tokens - (K - 1) :, :]
     tail_bc = bc_in[0, tokens - (K - 1) :, :]
@@ -121,7 +121,9 @@
         output_cols = lax.dynamic_slice_in_dim(values, G * N + group_start * N, span, 1)
         return jnp.concatenate([input_cols, output_cols], axis=1)
 
-    x_conv = causal_conv(prev_x, x_in[0], conv_x)
+    x_head = causal_conv(prev_x, x_in[0, : K - 1], conv_x)
+    x_rest = causal_conv(x_in[0, : K - 1].astype(jnp.float32), x_in[0, K - 1 :], conv_x)
+    x_conv = jnp.concatenate([x_head, x_rest], axis=0)
     bc_conv = causal_conv(pick_groups(prev_bc), pick_groups(bc_in[0]), pick_groups(conv_bc))
     positions = ctx_pos * tokens + lax.iota(jnp.int32, tokens)
     live_mask = (positions < lengths[req_pos]).astype(jnp.float32)
@@ -145,13 +147,17 @@
 
     chunk = local_heads // CHUNKS
     end_chunks = local_end.reshape(CHUNKS, chunk, P_SIZE, N)
+    init_chunks = first_state.reshape(CHUNKS, chunk, P_SIZE, N)
     decay_chunks = own_decay.reshape(CHUNKS, chunk)
     got = jnp.zeros((chunk, P_SIZE, N), jnp.float32)
     received = []
     for step in range(n_ctx + CHUNKS - 2):
         index = jnp.clip(step - ctx_pos, 0, CHUNKS - 1)
+        prior = jnp.where(
+            at_start, lax.dynamic_index_in_dim(init_chunks, index, keepdims=False), got
+        )
         sent = (
-            lax.dynamic_index_in_dim(decay_chunks, index, keepdims=False)[:, None, None] * got
+            lax.dynamic_index_in_dim(decay_chunks, index, keepdims=False)[:, None, None] * prior
             + lax.dynamic_index_in_dim(end_chunks, index, keepdims=False)
         )
         pairs = [
@@ -162,12 +168,7 @@
         received.append(got)
     received = jnp.stack(received)
     prefix = lax.dynamic_slice_in_dim(received, jnp.maximum(ctx_pos - 1, 0), CHUNKS, 0)
-    prefix = jnp.where(at_start, 0.0, prefix.reshape(local_heads, P_SIZE, N))
-
-    all_decay = lax.all_gather(own_decay, "ctx")
-    earlier = (lax.iota(jnp.int32, n_ctx) < ctx_pos)[:, None]
-    decay_before = jnp.prod(jnp.where(earlier, all_decay, 1.0), axis=0)
-    start_state = prefix + decay_before[:, None, None] * first_state
+    start_state = jnp.where(at_start, first_state, prefix.reshape(local_heads, P_SIZE, N))
     end_state = own_decay[:, None, None] * start_state + local_end
 
     outs = []

time: 271 us -> 253 us (0.934); the launches traced: 266 us -> 252 us
  blocking collectives: 36.4 us -> 0 us
  waiting for transfers between devices: 101 us -> 113 us
  local copies, waits for them, and re-layouts: 33.5 us -> 37.9 us
  matrix products: 16.5 us -> 19.6 us
    psum x1 -> x0, blocking collectives: 36.4 us -> none  [on_device(): lax.psum(jnp.where(on_chip, jnp.where(mine, conv_pool[0], other_conv), 0....]
    psum x1, waiting for transfers between devices: 41.1 us -> 50.5 us  [on_device(): picked = lax.psum(picked, 'ctx')]
    unnamed x151 -> x189, local copies, waits for them, and re-layouts: 23.4 us -> 15.6 us
    broadcast_in_dim x1 -> x0, other arithmetic: 3.53 us -> none  [on_device(): return (gated, end_state[None, None])]
    slice x2 -> x6, local copies, waits for them, and re-layouts: 0.2 us -> 3.5 us  [the longest x2 2.57 us: on_device(): first_state = picked[:state_pick.size].reshape(state_pick.shape)]
    optimization_barrier x0 -> x1, local copies, waits for them, and re-layouts: none -> 2.85 us  [on_device(): lax.optimization_barrier((picked, x_in, bc_in, dt_raw))]
    convert_element_type x2 -> x3, other arithmetic: 11.9 us -> 13.1 us  [causal_conv(): return jax.nn.silu(total).astype(jnp.bfloat16)]
  transfers between devices with their start and end apart: 15 -> 15, of which waited for: 5 -> 5; matrix products, arithmetic and copies ran while one was open for 31% -> 25% of each run, Pallas kernels for 0% -> 0%
where the time goes in v3:
time: 253 us; the launch traced here: 252 us
  waiting for transfers between devices  113 us (45%)
  other arithmetic  49.7 us (20%)
  local copies, waits for them, and re-layouts  37.9 us (15%)
  matrix products  19.6 us (8%)
  between operations  18.3 us (7%)
  starting transfers between devices  13.8 us (5%)
    ppermute x10, waiting for transfers between devices, on_device(): got = lax.ppermute(sent, 'ctx', pairs)  62.1 us
    psum x1, waiting for transfers between devices, on_device(): picked = lax.psum(picked, 'ctx')  50.5 us
    unnamed x189, local copies, waits for them, and re-layouts  15.6 us
    convert_element_type x3, other arithmetic, causal_conv(): return jax.nn.silu(total).astype(jnp.bfloat16)  13.1 us
    ppermute x10, starting transfers between devices, on_device(): got = lax.ppermute(sent, 'ctx', pairs)  10.4 us
    dot_general x4, matrix products, block_output(): jnp.einsum('hqs,shp->qhp', weights, x_blk, preferred_element_type=jnp.flo...  7.94 us
    another operation x5, other arithmetic  6.93 us
  transfers between devices with their start and end apart: 15, of which 5 were waited for; matrix products, arithmetic and copies ran while one was open for 25% of the time, Pallas kernels for 0%

profile of v3, /device:TPU:246, one launch (start us, length us, event | category | flops | bytes accessed | tf_op | source)
XLA Modules:
  0.0 251.7 jit_solution(4440000627590166594)
XLA Ops:
  7.3 0.7 copy.135
  8.6 1.2 dynamic_slice.132
  11.1 0.7 constant_dynamic-slice_fusion.14
  13.1 1.5 fusion.151
  14.6 1.2 fusion.127
  19.1 3.9 %copy.78 = bf16[1,1024,1024]{1,2,0:T(8,128)(2,1)} copy(bf16[1,1024,1024]{2,1,0:T(8,128)(2,1)} %param.16) | data formatting | bytes 4194304 | tf_op args[2]
  23.8 1.1 pad_maximum_fusion.2
  24.9 1.3 dynamic-slice_bitcast_fusion.1
  26.2 1.6 slice_bitcast_fusion.3
  27.7 2.9 %copy.66 = bf16[1,1024,1024]{1,2,0:T(8,128)(2,1)S(1)} copy(bf16[1,1024,1024]{2,1,0:T(8,128)(2,1)} %param.14) | data formatting | bytes 4194304 | tf_op jit(solution)/shard_map/optimization_barrier | solution.py:104
  30.6 1.3 slice_bitcast_fusion.4
  32.2 2.3 reduce-window.14
  40.1 0.7 exponential_bitcast_fusion
  41.4 1.3 collective-permute-start.3
  42.7 3.0 %fusion.21 = f32[1021,1024]{0,1:T(8,128)} fusion(bf16[1,1024,1024]{1,2,0:T(8,128)(2,1)S(1)} %copy.66), kind=kLoop, calls=%fused_computation.38 | loop fusion | flops 1045504 | bytes 6273024 | tf_op jit(solution)/shard_map/convert_element_type | solution.py:27
  45.6 1.0 copy.67
  46.7 1.5 collective-permute-start.2
  48.2 11.3 %multiply_convert_fusion.4 = bf16[1021,1024]{0,1:T(8,128)(2,1)S(1)} fusion(f32[1021,1024]{0,1:T(8,128)} %fusion.21, f32[3,1024]{0,1:T(8,128)} %copy.67, f32[1024]{0:T(1024)S(1)} %bitcast.440, f32[1024]{0:T(1024)S(1)} %bitcast.442, f32[1024]{0:T(1024)S(1)} %bitcast.438, f32[1024]{0:T(1024)S(1)} %bitcast.436), kind=kLoop, calls=%fused_computation.24 | loop fusion | flops 15682560 | bytes 6301696 | tf_op jit(solution)/shard_map/convert_element_type | solution.py:32
  59.5 1.9 fusion.148
  62.4 4.5 %reduce-window.16 = f32[16,8,128]{2,1,0:T(8,128)S(1)} reduce-window(f32[16,8,128]{2,1,0:T(8,128)S(1)} %fusion.116, f32[]{:T(128)} %constant.162.clone.1), window={size=1x1x128 pad=0_0x0_0x127_0}, to_apply=%region_4.5 | reduce-window | flops 2080768 | bytes 131076 | tf_op jit(solution)/shard_map/reduce-window.2
  67.4 1.6 maximum_convert_fusion
  72.3 1.9 pad_maximum_fusion.1
  74.2 1.2 multiply_convert_fusion.9
  75.5 1.1 fusion.102
  76.5 50.5 %all-reduce.2.cloned.1.call-done = f32[265216]{0:T(1024)} async-done(((f32[265216]{0:T(1024)}), f32[265216]{0:T(1024)}) %all-reduce.2.cloned.1.call-update) | async-done | bytes 1060880 | tf_op jit(solution)/shard_map/psum | solution.py:105
  127.0 0.7 slice.272
  128.4 0.9 copy.68
  129.3 2.9 %fusion.65 = (bf16[256,1024]{0,1:T(8,128)(2,1)S(1)}, bf16[256,1024]{0,1:T(8,128)(2,1)}, bf16[256,1024]{0,1:T(8,128)(2,1)S(1)}, bf16[256,1024]{0,1:T(8,128)(2,1)S(1)}, bf16[256,1024]{0,1:T(8,128)(2,1)S(1)}) fusion(f32[256,16]{0,1:T(8,128)S(1)} %get-tuple-element.52, bf16[1021,1024]{0,1:T(8,128)(2,1)S(1)} %multiply_convert_fusion.4, ...), kind=kLoop, calls=%fused_computation.94 | loop fusion | flops 4194304 | bytes 6619136 | tf_op jit(solution)/shard_map/convert_element_type | solution.py:41
  132.5 1.3 fusion.85
  134.1 1.3 fusion.79
  135.4 1.3 reshape_reshape.3
  136.8 2.1 multiply_add_fusion
  139.0 0.7 collective-permute-start.4
  139.8 1.4 fusion.48
  141.6 0.7 collective-permute-start.5
  142.3 2.6 %fusion.47 = f32[256,16,64]{0,2,1:T(8,128)} fusion(bf16[256,16,64]{0,2,1:T(8,128)(2,1)S(1)} %bitcast.410, f32[16,256]{1,0:T(8,128)S(1)} %copy-done.54, f32[16,256]{1,0:T(8,128)S(1)} %bitcast.433, f32[256,256]{1,0:T(8,128)S(1)} %fusion.97, pred[256,256]{1,0:T(8,128)(4,1)S(1)} %copy-done.37), kind=kOutput, calls=%fused_computation.65 | convolution fusion | flops 141557760 | bytes 1933312 | tf_op jit(solution)/shard_map/hqs,shp->qhp/dot_general | solution.py:64
  145.2 0.9 collective-permute-start.6
  146.2 2.6 %fusion.46 = f32[256,16,64]{0,2,1:T(8,128)} fusion(bf16[256,16,64]{0,2,1:T(8,128)(2,1)S(1)} %bitcast.414, f32[16,256]{1,0:T(8,128)S(1)} %copy-done.52, f32[16,256]{1,0:T(8,128)S(1)} %bitcast.429, f32[256,256]{1,0:T(8,128)S(1)} %fusion.92, pred[256,256]{1,0:T(8,128)(4,1)S(1)} %copy-done.37), kind=kOutput, calls=%fused_computation.64 | convolution fusion | flops 141557760 | bytes 1933312 | tf_op jit(solution)/shard_map/hqs,shp->qhp/dot_general | solution.py:64
  149.2 0.7 collective-permute-start.7
  149.9 1.4 fusion.49
  152.2 1.8 fusion.59
  154.0 0.8 bitcast_add_fusion.4
  154.8 1.4 collective-permute-start.9
  156.2 1.7 fusion.58
  157.9 2.5 slice.267
  160.4 1.2 bitcast_add_fusion.3
  161.7 1.3 collective-permute-start.10
  163.0 1.0 bitcast_dynamic-update-slice_fusion.8
  163.9 1.0 bitcast_dynamic-update-slice_fusion.7
  164.9 42.8 %collective-permute-done.10 = f32[4,64,256]{2,1,0:T(8,128)S(1)} collective-permute-done((f32[4,64,256]{2,1,0:T(8,128)S(1)}, f32[4,64,256]{2,1,0:T(8,128)S(1)}, u32[]{:S(2)}, u32[]{:S(2)}) %collective-permute-start.10) | collective-permute-done | bytes 262176 | tf_op jit(solution)/shard_map/ppermute | solution.py:167
  207.7 1.0 bitcast_add_fusion.2
  208.9 1.6 collective-permute-start.11
  210.4 1.0 bitcast_dynamic-update-slice_fusion.6
  211.4 6.3 %collective-permute-done.11 = f32[4,64,256]{2,1,0:T(8,128)S(1)} collective-permute-done((f32[4,64,256]{2,1,0:T(8,128)S(1)}, f32[4,64,256]{2,1,0:T(8,128)S(1)}, u32[]{:S(2)}, u32[]{:S(2)}) %collective-permute-start.11) | collective-permute-done | bytes 262176 | tf_op jit(solution)/shard_map/ppermute | solution.py:167
  217.9 1.3 collective-permute-start.12
  219.2 1.0 bitcast_dynamic-update-slice_fusion.4
  220.2 6.0 %collective-permute-done.12 = f32[4,64,256]{2,1,0:T(8,128)S(1)} collective-permute-done((f32[4,64,256]{2,1,0:T(8,128)S(1)}, f32[4,64,256]{2,1,0:T(8,128)S(1)}, u32[]{:S(2)}, u32[]{:S(2)}) %collective-permute-start.12) | collective-permute-done | bytes 262176 | tf_op jit(solution)/shard_map/ppermute | solution.py:167
  226.2 1.3 collective-permute-start.13
  227.6 6.9 %collective-permute-done.13 = f32[4,64,256]{2,1,0:T(8,128)S(1)} collective-permute-done((f32[4,64,256]{2,1,0:T(8,128)S(1)}, f32[4,64,256]{2,1,0:T(8,128)S(1)}, u32[]{:S(2)}, u32[]{:S(2)}) %collective-permute-start.13) | collective-permute-done | bytes 262176 | tf_op jit(solution)/shard_map/ppermute | solution.py:167
  234.7 1.6 add_bitcast_fusion
  236.3 1.8 fusion.67
  239.0 0.8 fusion.61
  240.4 1.9 fusion.13
  242.3 2.6 %copy.79 = bf16[1,1024,1024]{2,1,0:T(8,128)(2,1)} copy(bf16[1,1024,1024]{1,2,0:T(8,128)(2,1)S(1)} %fusion.13) | data formatting | bytes 4194304
  (266 shorter events, 20.5 us)
Async XLA Ops:
  7.2 8.6 %copy-start = (s32[2,1]{0,1:T(1,128)S(1)}, s32[2,1]{0,1:T(1,128)}, u32[]{:S(2)}) copy-start(s32[2,1]{0,1:T(1,128)} %param.26) | copy-start | bytes 28
  7.2 15.9 %copy-start.30 = (f32[1,16,64,256]{3,2,1,0:T(8,128)S(1)}, f32[1,16,64,256]{3,2,1,0:T(8,128)}, u32[]{:S(2)}) copy-start(f32[1,16,64,256]{3,2,1,0:T(8,128)} %param.23) | copy-start | bytes 3145732
  7.2 15.8 %copy-start.38 = (f32[1,3,1024]{2,0,1:T(1,128)S(1)}, f32[1,3,1024]{2,0,1:T(1,128)}, u32[]{:S(2)}) copy-start(f32[1,3,1024]{2,0,1:T(1,128)} %param.24) | copy-start | bytes 36868
  7.2 119.8 %all-reduce.2.cloned.1.call-start = ((), (), s32[]{:S(2)}) async-start(), calls=%async_computation | async-start | bytes 2121728 | tf_op jit(solution)/shard_map/psum | solution.py:105
  7.2 15.8 %collective-permute-start = (f32[16,64,256]{2,1,0:T(8,128)}, f32[16,64,256]{2,1,0:T(8,128)S(1)}, u32[]{:S(2)}, u32[]{:S(2)}) collective-permute-start(f32[16,64,256]{2,1,0:T(8,128)} %bitcast.416), channel_id=1, source_target_pairs={{0,1},{1,0},{2,3},{3,2},{4,5},{5,4},{6,7},{7,6},{8,9},{9,8},{10,11... | collective-permute-start | bytes 3145736 | tf_op jit(solution)/shard_map/ppermute | solution.py:100
  8.1 14.9 %collective-permute-start.1 = (f32[3,1024]{1,0:T(4,128)S(1)}, f32[3,1024]{1,0:T(4,128)S(1)}, u32[]{:S(2)}, u32[]{:S(2)}) collective-permute-start(f32[3,1024]{1,0:T(4,128)S(1)} %bitcast.445), channel_id=1, source_target_pairs={{0,1},{1,0},{2,3},{3,2},{4,5},{5,4},{6,7},{7,6},{8,9},{9,8},{10,11... | collective-permute-start | bytes 36872 | tf_op jit(solution)/shard_map/ppermute | solution.py:100
  23.7 8.2 %copy-start.33 = (f32[1,16,1024]{2,1,0:T(8,128)S(1)}, f32[1,16,1024]{2,1,0:T(8,128)}, u32[]{:S(2)}) copy-start(f32[1,16,1024]{2,1,0:T(8,128)} %param.17) | copy-start | bytes 196612
  23.8 8.2 %copy-start.64 = (f32[16]{0:T(128)S(1)}, f32[16]{0:T(128)}, u32[]{:S(2)}) copy-start(f32[16]{0:T(128)} %param.18) | copy-start | bytes 196
  23.8 8.2 %copy-start.66 = (f32[16]{0:T(128)S(1)}, f32[16]{0:T(128)}, u32[]{:S(2)}) copy-start(f32[16]{0:T(128)} %param.19) | copy-start | bytes 196
  26.1 41.2 %copy-start.11 = (bf16[1024,256]{1,0:T(8,128)(2,1)}, bf16[1024,256]{1,0:T(8,128)(2,1)S(1)}, u32[]{:S(2)}) copy-start(bf16[1024,256]{1,0:T(8,128)(2,1)S(1)} %get-tuple-element.27) | copy-start | bytes 1572868
  26.2 41.2 %copy-start.13 = (bf16[1024,256]{1,0:T(8,128)(2,1)}, bf16[1024,256]{1,0:T(8,128)(2,1)S(1)}, u32[]{:S(2)}) copy-start(bf16[1024,256]{1,0:T(8,128)(2,1)S(1)} %get-tuple-element.28) | copy-start | bytes 1572868
  36.8 11.4 %copy-start.48 = (f32[1,1024]{1,0:T(1,128)S(1)}, f32[1,1024]{1,0:T(1,128)}, u32[]{:S(2)}) copy-start(f32[1,1024]{1,0:T(1,128)} %get-tuple-element.61) | copy-start | bytes 12292
  36.8 11.4 %copy-start.49 = (f32[1,1024]{1,0:T(1,128)S(1)}, f32[1,1024]{1,0:T(1,128)}, u32[]{:S(2)}) copy-start(f32[1,1024]{1,0:T(1,128)} %get-tuple-element.62) | copy-start | bytes 12292
  41.4 30.8 %collective-permute-start.3 = (bf16[3,4096]{1,0:T(4,128)(2,1)}, bf16[3,4096]{1,0:T(4,128)(2,1)S(1)}, u32[]{:S(2)}, u32[]{:S(2)}) collective-permute-start(bf16[3,4096]{1,0:T(4,128)(2,1)} %slice_bitcast_fusion.3), channel_id=1, source_target_pairs={{0,32},{32,64},{64,96},{96,128},{128,160},{160,192},{192,224},{1,3... | collective-permute-start | bytes 73736 | tf_op jit(solution)/shard_map/ppermute | solution.py:23
  46.7 81.0 %collective-permute-start.2 = (bf16[3,1024]{1,0:T(4,128)(2,1)}, bf16[3,1024]{1,0:T(4,128)(2,1)S(1)}, u32[]{:S(2)}, u32[]{:S(2)}) collective-permute-start(bf16[3,1024]{1,0:T(4,128)(2,1)} %get-tuple-element.35), channel_id=1, source_target_pairs={{0,32},{32,64},{64,96},{96,128},{128,160},{160,192},{192,224},{1,3... | collective-permute-start | bytes 18440 | tf_op jit(solution)/shard_map/ppermute | solution.py:23
  48.2 13.2 %copy-start.65 = (f32[16]{0:T(128)S(1)}, f32[16]{0:T(128)}, u32[]{:S(2)}) copy-start(f32[16]{0:T(128)} %param.18) | copy-start | bytes 196
  48.2 13.2 %copy-start.67 = (f32[16]{0:T(128)S(1)}, f32[16]{0:T(128)}, u32[]{:S(2)}) copy-start(f32[16]{0:T(128)} %param.19) | copy-start | bytes 196
  48.2 14.1 %copy-start.50 = (f32[8,128]{1,0:T(8,128)S(1)}, f32[8,128]{1,0:T(8,128)}, u32[]{:S(2)}) copy-start(f32[8,128]{1,0:T(8,128)} %fusion.127) | copy-start | bytes 12292
  59.5 12.7 %copy-start.39 = (f32[1,3,4096]{2,0,1:T(1,128)S(1)}, f32[1,3,4096]{2,0,1:T(1,128)}, u32[]{:S(2)}) copy-start(f32[1,3,4096]{2,0,1:T(1,128)} %param.25) | copy-start | bytes 147460
  62.3 11.9 %copy-start.59 = (f32[1,512]{1,0:T(1,128)S(1)}, f32[1,512]{1,0:T(1,128)}, u32[]{:S(2)}) copy-start(f32[1,512]{1,0:T(1,128)} %get-tuple-element.63) | copy-start | bytes 6148
  62.3 11.9 %copy-start.60 = (f32[1,512]{1,0:T(1,128)S(1)}, f32[1,512]{1,0:T(1,128)}, u32[]{:S(2)}) copy-start(f32[1,512]{1,0:T(1,128)} %get-tuple-element.64) | copy-start | bytes 6148
  62.3 11.9 %copy-start.61 = (f32[1,512]{1,0:T(1,128)S(1)}, f32[1,512]{1,0:T(1,128)}, u32[]{:S(2)}) copy-start(f32[1,512]{1,0:T(1,128)} %get-tuple-element.65) | copy-start | bytes 6148
  62.3 11.9 %copy-start.62 = (f32[1,512]{1,0:T(1,128)S(1)}, f32[1,512]{1,0:T(1,128)}, u32[]{:S(2)}) copy-start(f32[1,512]{1,0:T(1,128)} %get-tuple-element.66) | copy-start | bytes 6148
  75.5 58.6 %copy-start.4 = (bf16[1024,512]{1,0:T(8,128)(2,1)}, bf16[1024,512]{1,0:T(8,128)(2,1)S(1)}, u32[]{:S(2)}) copy-start(bf16[1024,512]{1,0:T(8,128)(2,1)S(1)} %multiply_convert_fusion.9) | copy-start | bytes 3145732
  132.2 3.2 %copy-start.24 = (f32[265216]{0:T(1024)S(1)}, f32[265216]{0:T(1024)}, u32[]{:S(2)}) copy-start(f32[265216]{0:T(1024)} %all-reduce.2.cloned.1.call-done) | copy-start | bytes 3182596
  133.8 3.1 %copy-start.55 = (f32[4,4]{1,0:T(4,128)S(1)}, f32[4,4]{1,0:T(4,128)}, u32[]{:S(2)}) copy-start(f32[4,4]{1,0:T(4,128)} %exp.155) | copy-start | bytes 196
  133.8 3.1 %copy-start.56 = (f32[4,4]{1,0:T(4,128)S(1)}, f32[4,4]{1,0:T(4,128)}, u32[]{:S(2)}) copy-start(f32[4,4]{1,0:T(4,128)} %exp.157) | copy-start | bytes 196
  133.8 3.1 %copy-start.57 = (f32[4,4]{1,0:T(4,128)S(1)}, f32[4,4]{1,0:T(4,128)}, u32[]{:S(2)}) copy-start(f32[4,4]{1,0:T(4,128)} %exp.159) | copy-start | bytes 196
  133.8 3.1 %copy-start.58 = (f32[4,4]{1,0:T(4,128)S(1)}, f32[4,4]{1,0:T(4,128)}, u32[]{:S(2)}) copy-start(f32[4,4]{1,0:T(4,128)} %mul.667) | copy-start | bytes 196
  135.4 3.5 %copy-start.82 = (f32[4]{0:T(128)S(1)}, f32[4]{0:T(128)}, u32[]{:S(2)}) copy-start(f32[4]{0:T(128)} %get-tuple-element.76) | copy-start | bytes 52
  135.4 4.3 %copy-start.47 = (f32[2,8,2,128]{3,1,2,0:T(8,128)S(1)}, f32[2,8,2,128]{3,1,2,0:T(8,128)}, u32[]{:S(2)}) copy-start(f32[2,8,2,128]{3,1,2,0:T(8,128)} %copy-done.46) | copy-start | bytes 49156
  136.8 3.0 %copy-start.53 = (f32[16,256]{1,0:T(8,128)S(1)}, f32[16,256]{1,0:T(8,128)}, u32[]{:S(2)}) copy-start(f32[16,256]{1,0:T(8,128)} %get-tuple-element.79) | copy-start | bytes 49156
  139.0 2.4 collective-permute-start.4
  141.6 3.5 %collective-permute-start.5 = (f32[4,64,256]{2,1,0:T(8,128)S(1)}, f32[4,64,256]{2,1,0:T(8,128)S(1)}, u32[]{:S(2)}, u32[]{:S(2)}) collective-permute-start(f32[4,64,256]{2,1,0:T(8,128)S(1)} %bitcast_add_fusion.8), channel_id=1, source_target_pairs={{0,32},{32,64},{1,33},{33,65},{2,34},{34,66},{3,35},{35,67},{4,36}... | collective-permute-start | bytes 786440 | tf_op jit(solution)/shard_map/ppermute | solution.py:167
  142.3 3.8 %copy-start.22 = (bf16[256,1024]{0,1:T(8,128)(2,1)S(1)}, bf16[256,1024]{0,1:T(8,128)(2,1)}, u32[]{:S(2)}) copy-start(bf16[256,1024]{0,1:T(8,128)(2,1)} %get-tuple-element.30) | copy-start | bytes 1572868
  142.3 3.8 %copy-start.41 = (f32[2,8,2,128]{3,1,2,0:T(8,128)S(1)}, f32[2,8,2,128]{3,1,2,0:T(8,128)}, u32[]{:S(2)}) copy-start(f32[2,8,2,128]{3,1,2,0:T(8,128)} %copy-done.40) | copy-start | bytes 49156
  142.3 3.8 %copy-start.52 = (f32[16,256]{1,0:T(8,128)S(1)}, f32[16,256]{1,0:T(8,128)}, u32[]{:S(2)}) copy-start(f32[16,256]{1,0:T(8,128)} %get-tuple-element.77) | copy-start | bytes 49156
  145.1 3.7 %copy-start.25 = (f32[4,64,256]{2,1,0:T(8,128)}, f32[4,64,256]{2,1,0:T(8,128)S(1)}, u32[]{:S(2)}) copy-start(f32[4,64,256]{2,1,0:T(8,128)S(1)} %collective-permute-done.5) | copy-start | bytes 786436
  145.2 3.8 %collective-permute-start.6 = (f32[4,64,256]{2,1,0:T(8,128)S(1)}, f32[4,64,256]{2,1,0:T(8,128)S(1)}, u32[]{:S(2)}, u32[]{:S(2)}) collective-permute-start(f32[4,64,256]{2,1,0:T(8,128)S(1)} %bitcast_add_fusion.7), channel_id=1, source_target_pairs={{0,32},{32,64},{64,96},{1,33},{33,65},{65,97},{2,34},{34,66},{66,9... | collective-permute-start | bytes 786440 | tf_op jit(solution)/shard_map/ppermute | solution.py:167
  146.2 3.7 %copy-start.18 = (bf16[256,1024]{0,1:T(8,128)(2,1)S(1)}, bf16[256,1024]{0,1:T(8,128)(2,1)}, u32[]{:S(2)}) copy-start(bf16[256,1024]{0,1:T(8,128)(2,1)} %get-tuple-element.26) | copy-start | bytes 1572868
  146.2 3.7 %copy-start.43 = (f32[2,8,2,128]{3,1,2,0:T(8,128)S(1)}, f32[2,8,2,128]{3,1,2,0:T(8,128)}, u32[]{:S(2)}) copy-start(f32[2,8,2,128]{3,1,2,0:T(8,128)} %copy-done.42) | copy-start | bytes 49156
  146.2 3.7 %copy-start.51 = (f32[16,256]{1,0:T(8,128)S(1)}, f32[16,256]{1,0:T(8,128)}, u32[]{:S(2)}) copy-start(f32[16,256]{1,0:T(8,128)} %get-tuple-element.80) | copy-start | bytes 49156
  149.2 2.2 collective-permute-start.7
  151.3 3.5 %copy-start.27 = (f32[4,64,256]{2,1,0:T(8,128)}, f32[4,64,256]{2,1,0:T(8,128)S(1)}, u32[]{:S(2)}) copy-start(f32[4,64,256]{2,1,0:T(8,128)S(1)} %collective-permute-done.7) | copy-start | bytes 786436
  151.4 2.5 %collective-permute-start.8 = (f32[4,64,256]{2,1,0:T(8,128)S(1)}, f32[4,64,256]{2,1,0:T(8,128)S(1)}, u32[]{:S(2)}, u32[]{:S(2)}) collective-permute-start(f32[4,64,256]{2,1,0:T(8,128)S(1)} %bitcast_add_fusion.5), channel_id=1, source_target_pairs={{32,64},{64,96},{96,128},{128,160},{33,65},{65,97},{97,129},{129,1... | collective-permute-start | bytes 786440 | tf_op jit(solution)/shard_map/ppermute | solution.py:167
  152.2 8.3 %copy-start.74 = (f32[4]{0:T(128)S(1)}, f32[4]{0:T(128)}, u32[]{:S(2)}) copy-start(f32[4]{0:T(128)} %get-tuple-element.70) | copy-start | bytes 52
  154.0 53.8 %copy-start.73 = (f32[4]{0:T(128)S(1)}, f32[4]{0:T(128)}, u32[]{:S(2)}) copy-start(f32[4]{0:T(128)} %get-tuple-element.69) | copy-start | bytes 52
  154.8 5.6 %collective-permute-start.9 = (f32[4,64,256]{2,1,0:T(8,128)}, f32[4,64,256]{2,1,0:T(8,128)}, u32[]{:S(2)}, u32[]{:S(2)}) collective-permute-start(f32[4,64,256]{2,1,0:T(8,128)} %bitcast_add_fusion.4), channel_id=1, source_target_pairs={{64,96},{96,128},{128,160},{160,192},{65,97},{97,129},{129,161},{1... | collective-permute-start | bytes 786440 | tf_op jit(solution)/shard_map/ppermute | solution.py:167
  156.2 61.6 %copy-start.72 = (f32[4]{0:T(128)S(1)}, f32[4]{0:T(128)}, u32[]{:S(2)}) copy-start(f32[4]{0:T(128)} %get-tuple-element.68) | copy-start | bytes 52
  157.9 68.3 %copy-start.71 = (f32[4]{0:T(128)S(1)}, f32[4]{0:T(128)}, u32[]{:S(2)}) copy-start(f32[4]{0:T(128)} %get-tuple-element.67) | copy-start | bytes 52
  160.4 51.0 %copy-start.29 = (f32[4,64,256]{2,1,0:T(8,128)S(1)}, f32[4,64,256]{2,1,0:T(8,128)}, u32[]{:S(2)}) copy-start(f32[4,64,256]{2,1,0:T(8,128)} %copy-done.28) | copy-start | bytes 786436
  160.4 57.4 %copy-start.3 = (f32[4,4,64,256]{3,2,1,0:T(8,128)S(1)}, f32[4,4,64,256]{3,2,1,0:T(8,128)}, u32[]{:S(2)}) copy-start(f32[4,4,64,256]{3,2,1,0:T(8,128)} %reshape_reshape.3) | copy-start | bytes 3145732
  161.7 46.1 %collective-permute-start.10 = (f32[4,64,256]{2,1,0:T(8,128)S(1)}, f32[4,64,256]{2,1,0:T(8,128)S(1)}, u32[]{:S(2)}, u32[]{:S(2)}) collective-permute-start(f32[4,64,256]{2,1,0:T(8,128)S(1)} %bitcast_add_fusion.3), channel_id=1, source_target_pairs={{96,128},{128,160},{160,192},{192,224},{97,129},{129,161},{161,193... | collective-permute-start | bytes 786440 | tf_op jit(solution)/shard_map/ppermute | solution.py:167
  208.8 25.8 %copy-start.8 = (f32[16,64,256]{2,1,0:T(8,128)S(1)}, f32[16,64,256]{2,1,0:T(8,128)}, u32[]{:S(2)}) copy-start(f32[16,64,256]{2,1,0:T(8,128)} %fusion.85) | copy-start | bytes 3145732
  208.8 25.8 %copy-start.9 = (f32[16,64,256]{2,1,0:T(8,128)S(1)}, f32[16,64,256]{2,1,0:T(8,128)}, u32[]{:S(2)}) copy-start(f32[16,64,256]{2,1,0:T(8,128)} %fusion.79) | copy-start | bytes 3145732
  208.8 25.8 %copy-start.17 = (f32[16,64,256]{2,1,0:T(8,128)S(1)}, f32[16,64,256]{2,1,0:T(8,128)}, u32[]{:S(2)}) copy-start(f32[16,64,256]{2,1,0:T(8,128)} %slice.267) | copy-start | bytes 3145732
  208.8 25.8 %copy-start.70 = (f32[16]{0:T(128)S(1)}, f32[16]{0:T(128)}, u32[]{:S(2)}) copy-start(f32[16]{0:T(128)} %copy-done.69) | copy-start | bytes 196
  208.8 25.8 %copy-start.80 = (f32[16]{0:T(128)S(1)}, f32[16]{0:T(128)}, u32[]{:S(2)}) copy-start(f32[16]{0:T(128)} %get-tuple-element.83) | copy-start | bytes 196
  208.8 25.8 %copy-start.81 = (f32[16]{0:T(128)S(1)}, f32[16]{0:T(128)}, u32[]{:S(2)}) copy-start(f32[16]{0:T(128)} %get-tuple-element.84) | copy-start | bytes 196
  208.8 25.8 %copy-start.83 = (f32[16]{0:T(128)S(1)}, f32[16]{0:T(128)}, u32[]{:S(2)}) copy-start(f32[16]{0:T(128)} %negate_exponential_fusion.3) | copy-start | bytes 196
  208.9 8.9 %collective-permute-start.11 = (f32[4,64,256]{2,1,0:T(8,128)S(1)}, f32[4,64,256]{2,1,0:T(8,128)S(1)}, u32[]{:S(2)}, u32[]{:S(2)}) collective-permute-start(f32[4,64,256]{2,1,0:T(8,128)S(1)} %bitcast_add_fusion.2), channel_id=1, source_target_pairs={{128,160},{160,192},{192,224},{129,161},{161,193},{193,225},{130,1... | collective-permute-start | bytes 786440 | tf_op jit(solution)/shard_map/ppermute | solution.py:167
  217.9 8.3 %collective-permute-start.12 = (f32[4,64,256]{2,1,0:T(8,128)S(1)}, f32[4,64,256]{2,1,0:T(8,128)S(1)}, u32[]{:S(2)}, u32[]{:S(2)}) collective-permute-start(f32[4,64,256]{2,1,0:T(8,128)S(1)} %bitcast_add_fusion.1), channel_id=1, source_target_pairs={{160,192},{192,224},{161,193},{193,225},{162,194},{194,226},{163,1... | collective-permute-start | bytes 786440 | tf_op jit(solution)/shard_map/ppermute | solution.py:167
  226.2 8.3 %collective-permute-start.13 = (f32[4,64,256]{2,1,0:T(8,128)S(1)}, f32[4,64,256]{2,1,0:T(8,128)S(1)}, u32[]{:S(2)}, u32[]{:S(2)}) collective-permute-start(f32[4,64,256]{2,1,0:T(8,128)S(1)} %bitcast_add_fusion), channel_id=1, source_target_pairs={{192,224},{193,225},{194,226},{195,227},{196,228},{197,229},{198,2... | collective-permute-start | bytes 786440 | tf_op jit(solution)/shard_map/ppermute | solution.py:167
  240.4 4.5 %copy-start.1 = (s32[2,1]{0,1:T(1,128)S(1)}, s32[2,1]{0,1:T(1,128)}, u32[]{:S(2)}) copy-start(s32[2,1]{0,1:T(1,128)} %param.26) | copy-start | bytes 28
  (35 other events, 70.0 us)
Sparse Core Ops, SparseCore 0:
  48.3 78.6 all-reduce.1
